TPU v7x, 512 devices: a whole 4x4x16 slice. The times are simulated.
512 devices in a mesh: ctx: 32 (over x, y, core), head: 16 (over z).
Axes of the slice: x: 4, y: 4, z: 16, core: 2. Of those that a mesh axis runs over, the one named last changes fastest.
Arguments:
- q_linear: bfloat16 [8192, 8192], P('ctx', 'head'), may hold values from -4 to 4
- k_linear: bfloat16 [8192, 8192], P('ctx', 'head'), may hold values from -4 to 4
- v_linear: bfloat16 [8192, 8192], P('ctx', 'head'), may hold values from -40 to 40
- log_decay: float32 [8192, 64], P('ctx', 'head'), may hold values from -1 to 0
- norm_gain: float32 [8192], P('head'), may hold values from 0.5 to 1.5
- q_soft: bfloat16 [8192, 8192], P('ctx', 'head'), may hold values from -6 to 6
- k_soft: bfloat16 [8192, 1024], P('ctx'), may hold values from -4 to 4
- v_soft: bfloat16 [8192, 1024], P('ctx'), may hold values from -4 to 4
Outputs:
- linear_out: bfloat16 [8192, 8192], P('ctx', 'head')
- soft_out: bfloat16 [8192, 8192], P('ctx', 'head')
All inputs are finite; a program needn't handle non-finite values.
Results may differ from a plain program's by a relative error of at most 0.0075.
Values may be sent and summed in bfloat16 or wider, within the bound.
No kernel may reach another device: no remote copies, remote signals or barrier semaphores. Data moves between devices by JAX's collectives and lax.ppermute only.
A program may use at most 64 MiB of HBM per device.

v0:
```python
import jax
import jax.numpy as jnp
from jax import lax
from jax.sharding import PartitionSpec as P

QUERY_HEADS = 64
DH = 128
KV_HEADS = 8
BLOCK = 256


EPSILON = 1e-06
NEGATIVE = -1e30


def shifted(value, axis, steps):
    count = lax.axis_size(axis)
    first, last = (max(0, -steps), min(count, count - steps))
    return lax.ppermute(value, axis, [(source, source + steps) for source in range(first, last)])


def lightning_step(carry, inputs):
    running, log_before = carry
    queries, key_rows, value_rows, log_gates = inputs
    row_count = queries.shape[0]
    cumulative = jnp.cumsum(log_gates, axis=0)
    final_log = cumulative[-1]
    positions = jnp.arange(row_count, dtype=jnp.int32)
    causal = positions[None, :] <= positions[:, None]
    cum_heads = cumulative.T
    log_gap = jnp.where(causal[None], cum_heads[:, :, None] - cum_heads[:, None, :], NEGATIVE)
    scores = jnp.einsum("thd,shd->hts", queries, key_rows, preferred_element_type=jnp.float32)
    weights = (scores * jnp.exp(log_gap)).astype(jnp.bfloat16)
    intra_part = jnp.einsum("hts,she->the", weights, value_rows, preferred_element_type=jnp.float32)
    query_wide = queries.astype(jnp.float32)
    lifted_here = query_wide * jnp.exp(cumulative)[:, :, None]
    carried_here = jnp.einsum("thd,hde->the", lifted_here, running, precision=lax.Precision.HIGHEST)
    lifted_device = query_wide * jnp.exp(cumulative + log_before[None, :])[:, :, None]
    scaled = (key_rows * jnp.exp(final_log[None, :] - cumulative)[:, :, None]).astype(jnp.bfloat16)
    block_state = jnp.einsum("shd,she->hde", scaled, value_rows, preferred_element_type=jnp.float32)
    running = jnp.exp(final_log)[:, None, None] * running + block_state
    return ((running, log_before + final_log), (intra_part + carried_here, lifted_device))


def soft_update(running, queries, query_pos, key_rows, value_rows, key_pos):
    row_max, row_total, weighted = running
    head_count, row_count = row_max.shape
    kv_count, group_local = (queries.shape[1], queries.shape[2])
    scores = jnp.einsum("tkgd,skd->kgts", queries, key_rows, preferred_element_type=jnp.float32)
    scores = scores.reshape(head_count, row_count, key_rows.shape[0]) * DH ** (-0.5)
    allowed = key_pos[None, :] <= query_pos[:, None]
    scores = jnp.where(allowed[None], scores, NEGATIVE)
    new_max = jnp.maximum(row_max, jnp.max(scores, axis=2))
    probabilities = jnp.where(allowed[None], jnp.exp(scores - new_max[:, :, None]), 0.0)
    rescale = jnp.exp(row_max - new_max)
    row_total = row_total * rescale + jnp.sum(probabilities, axis=2)
    rounded = probabilities.astype(jnp.bfloat16).reshape(
        kv_count, group_local, row_count, key_rows.shape[0]
    )
    product = jnp.einsum(
        "kgts,ske->kgte", rounded, value_rows, preferred_element_type=jnp.float32
    ).reshape(head_count, row_count, DH)
    weighted = weighted * rescale[:, :, None] + product
    return (new_max, row_total, weighted)


def over_blocks(running, pieces, row_count, visitor):
    key_rows, value_rows = pieces

    def one_block(block_index, inner_state):
        block_start = block_index * row_count
        keys_here = lax.dynamic_slice_in_dim(key_rows, block_start, row_count, 0)
        values_here = lax.dynamic_slice_in_dim(value_rows, block_start, row_count, 0)
        return visitor(inner_state, keys_here, values_here, block_start)

    return lax.fori_loop(0, key_rows.shape[0] // row_count, one_block, running)


def finish(row_total, weighted, row_count, width):
    return (
        jnp.transpose(weighted / row_total[:, :, None], (1, 0, 2))
        .reshape(row_count, width)
        .astype(jnp.bfloat16)
    )


def local(q_linear, k_linear, v_linear, log_decay, norm_gain, q_soft, k_soft, v_soft):
    row_count = q_linear.shape[0]
    head_count = log_decay.shape[1]
    width = head_count * DH
    local_blocks = row_count // BLOCK
    lin_shape = (local_blocks, BLOCK, head_count, DH)
    sequences = (
        q_linear.reshape(lin_shape),
        k_linear.reshape(lin_shape),
        v_linear.reshape(lin_shape),
        log_decay.reshape(local_blocks, BLOCK, head_count),
    )
    start_carry = (
        jnp.zeros((head_count, DH, DH), jnp.float32),
        jnp.zeros((head_count,), jnp.float32),
    )
    (block_state, log_total), (local_part, lifted) = lax.scan(
        lightning_step, start_carry, sequences
    )
    local_part = local_part.reshape(row_count, head_count, DH)
    lifted = lifted.reshape(row_count, head_count, DH)
    block_fade = jnp.exp(log_total)

    def advance(step_index, entering):
        leaving = block_fade[:, None, None] * entering + block_state
        return shifted(leaving, "ctx", 1)

    entering = lax.fori_loop(0, lax.axis_size("ctx") - 1, advance, jnp.zeros_like(block_state))
    carried = jnp.einsum("thd,hde->the", lifted, entering, precision=lax.Precision.HIGHEST)
    mixed = (local_part + carried).reshape(row_count, width)
    power = lax.psum(jnp.sum(mixed * mixed, axis=1), "head") / (QUERY_HEADS * DH)
    linear_out = (mixed * lax.rsqrt(power + EPSILON)[:, None] * norm_gain[None, :]).astype(
        jnp.bfloat16
    )
    group_size = QUERY_HEADS // KV_HEADS
    kv_count = max(1, head_count // group_size)
    group_local = head_count // kv_count
    kv_start = lax.axis_index("head") * head_count // group_size
    k_local = lax.dynamic_slice_in_dim(k_soft, kv_start * DH, kv_count * DH, 1)
    v_local = lax.dynamic_slice_in_dim(v_soft, kv_start * DH, kv_count * DH, 1)
    query_shape = (row_count, kv_count, group_local, DH)
    key_shape = (row_count, kv_count, DH)
    my_index = lax.axis_index("ctx")
    positions = jnp.arange(row_count, dtype=jnp.int32)
    initial = (
        jnp.full((head_count, row_count), NEGATIVE, jnp.float32),
        jnp.zeros((head_count, row_count), jnp.float32),
        jnp.zeros((head_count, row_count, DH), jnp.float32),
    )
    queries = q_soft.reshape(query_shape)
    query_pos = my_index * row_count + positions
    query_end = my_index * row_count + row_count - 1

    def visitor(running, keys_here, values_here, block_start):
        return lax.cond(
            block_start <= query_end,
            lambda state: soft_update(
                state,
                queries,
                query_pos,
                keys_here.reshape(key_shape),
                values_here.reshape(key_shape),
                block_start + positions,
            ),
            lambda state: state,
            running,
        )

    row_max, row_total, weighted = over_blocks(
        initial,
        (
            lax.all_gather(k_local, "ctx", axis=0, tiled=True),
            lax.all_gather(v_local, "ctx", axis=0, tiled=True),
        ),
        row_count,
        visitor,
    )
    soft_out = finish(row_total, weighted, row_count, width)
    return (linear_out, soft_out)


def solution(mesh):
    return jax.shard_map(
        local,
        mesh=mesh,
        in_specs=(
            P("ctx", "head"),
            P("ctx", "head"),
            P("ctx", "head"),
            P("ctx", "head"),
            P("head"),
            P("ctx", "head"),
            P("ctx", None),
            P("ctx", None),
        ),
        out_specs=(P("ctx", "head"), P("ctx", "head")),
        check_vma=False,
    )
```

profile of v0, /device:TPU:6, one launch (start us, length us, event | category | flops | bytes accessed | tf_op | source)
XLA Modules:
  0.0 451.1 jit_solution(13501809953526398341)
XLA Ops:
  16.4 310.2 %while.9 = (s32[]{:T(128)}, f32[4,128,128]{2,1,0:T(8,128)S(1)}, f32[4]{0:T(128)S(1)}, f32[4,128,128]{2,1,0:T(8,128)S(1)}, s32[]{:T(128)}) while((s32[]{:T(128)}, f32[4,128,128]{2,1,0:T(8,128)S(1)}, f32[4]{0:T(128)S(1)}, f32[4,128,128]{2,1,0:T(8,128)S(1)}, s32[]{:T(128)}) %tuple.85), condition=%wide.region_3.4_spmd, body=%wide.region_2.3_spmd.sunk | while | flops 131074 | bytes 1835125 | solution.py:114
  18.5 7.9 %collective-permute-done = f32[4,128,128]{2,1,0:T(8,128)S(1)} collective-permute-done((f32[4,128,128]{2,1,0:T(8,128)S(1)}, f32[4,128,128]{2,1,0:T(8,128)S(1)}, u32[]{:S(2)}, u32[]{:S(2)}) %collective-permute-start) | collective-permute-done | bytes 262176 | tf_op jit(solution)/shard_map/while/body/eval_jaxpr/ppermute | solution.py:19
  28.4 7.9 %collective-permute-done = f32[4,128,128]{2,1,0:T(8,128)S(1)} collective-permute-done((f32[4,128,128]{2,1,0:T(8,128)S(1)}, f32[4,128,128]{2,1,0:T(8,128)S(1)}, u32[]{:S(2)}, u32[]{:S(2)}) %collective-permute-start) | collective-permute-done | bytes 262176 | tf_op jit(solution)/shard_map/while/body/eval_jaxpr/ppermute | solution.py:19
  38.3 8.0 %collective-permute-done = f32[4,128,128]{2,1,0:T(8,128)S(1)} collective-permute-done((f32[4,128,128]{2,1,0:T(8,128)S(1)}, f32[4,128,128]{2,1,0:T(8,128)S(1)}, u32[]{:S(2)}, u32[]{:S(2)}) %collective-permute-start) | collective-permute-done | bytes 262176 | tf_op jit(solution)/shard_map/while/body/eval_jaxpr/ppermute | solution.py:19
  48.3 7.9 %collective-permute-done = f32[4,128,128]{2,1,0:T(8,128)S(1)} collective-permute-done((f32[4,128,128]{2,1,0:T(8,128)S(1)}, f32[4,128,128]{2,1,0:T(8,128)S(1)}, u32[]{:S(2)}, u32[]{:S(2)}) %collective-permute-start) | collective-permute-done | bytes 262176 | tf_op jit(solution)/shard_map/while/body/eval_jaxpr/ppermute | solution.py:19
  58.2 8.4 %collective-permute-done = f32[4,128,128]{2,1,0:T(8,128)S(1)} collective-permute-done((f32[4,128,128]{2,1,0:T(8,128)S(1)}, f32[4,128,128]{2,1,0:T(8,128)S(1)}, u32[]{:S(2)}, u32[]{:S(2)}) %collective-permute-start) | collective-permute-done | bytes 262176 | tf_op jit(solution)/shard_map/while/body/eval_jaxpr/ppermute | solution.py:19
  68.6 8.7 %collective-permute-done = f32[4,128,128]{2,1,0:T(8,128)S(1)} collective-permute-done((f32[4,128,128]{2,1,0:T(8,128)S(1)}, f32[4,128,128]{2,1,0:T(8,128)S(1)}, u32[]{:S(2)}, u32[]{:S(2)}) %collective-permute-start) | collective-permute-done | bytes 262176 | tf_op jit(solution)/shard_map/while/body/eval_jaxpr/ppermute | solution.py:19
  79.4 7.9 %collective-permute-done = f32[4,128,128]{2,1,0:T(8,128)S(1)} collective-permute-done((f32[4,128,128]{2,1,0:T(8,128)S(1)}, f32[4,128,128]{2,1,0:T(8,128)S(1)}, u32[]{:S(2)}, u32[]{:S(2)}) %collective-permute-start) | collective-permute-done | bytes 262176 | tf_op jit(solution)/shard_map/while/body/eval_jaxpr/ppermute | solution.py:19
  89.3 7.9 %collective-permute-done = f32[4,128,128]{2,1,0:T(8,128)S(1)} collective-permute-done((f32[4,128,128]{2,1,0:T(8,128)S(1)}, f32[4,128,128]{2,1,0:T(8,128)S(1)}, u32[]{:S(2)}, u32[]{:S(2)}) %collective-permute-start) | collective-permute-done | bytes 262176 | tf_op jit(solution)/shard_map/while/body/eval_jaxpr/ppermute | solution.py:19
  99.2 8.3 %collective-permute-done = f32[4,128,128]{2,1,0:T(8,128)S(1)} collective-permute-done((f32[4,128,128]{2,1,0:T(8,128)S(1)}, f32[4,128,128]{2,1,0:T(8,128)S(1)}, u32[]{:S(2)}, u32[]{:S(2)}) %collective-permute-start) | collective-permute-done | bytes 262176 | tf_op jit(solution)/shard_map/while/body/eval_jaxpr/ppermute | solution.py:19
  109.5 7.9 %collective-permute-done = f32[4,128,128]{2,1,0:T(8,128)S(1)} collective-permute-done((f32[4,128,128]{2,1,0:T(8,128)S(1)}, f32[4,128,128]{2,1,0:T(8,128)S(1)}, u32[]{:S(2)}, u32[]{:S(2)}) %collective-permute-start) | collective-permute-done | bytes 262176 | tf_op jit(solution)/shard_map/while/body/eval_jaxpr/ppermute | solution.py:19
  119.4 7.9 %collective-permute-done = f32[4,128,128]{2,1,0:T(8,128)S(1)} collective-permute-done((f32[4,128,128]{2,1,0:T(8,128)S(1)}, f32[4,128,128]{2,1,0:T(8,128)S(1)}, u32[]{:S(2)}, u32[]{:S(2)}) %collective-permute-start) | collective-permute-done | bytes 262176 | tf_op jit(solution)/shard_map/while/body/eval_jaxpr/ppermute | solution.py:19
  129.3 9.3 %collective-permute-done = f32[4,128,128]{2,1,0:T(8,128)S(1)} collective-permute-done((f32[4,128,128]{2,1,0:T(8,128)S(1)}, f32[4,128,128]{2,1,0:T(8,128)S(1)}, u32[]{:S(2)}, u32[]{:S(2)}) %collective-permute-start) | collective-permute-done | bytes 262176 | tf_op jit(solution)/shard_map/while/body/eval_jaxpr/ppermute | solution.py:19
  140.6 7.9 %collective-permute-done = f32[4,128,128]{2,1,0:T(8,128)S(1)} collective-permute-done((f32[4,128,128]{2,1,0:T(8,128)S(1)}, f32[4,128,128]{2,1,0:T(8,128)S(1)}, u32[]{:S(2)}, u32[]{:S(2)}) %collective-permute-start) | collective-permute-done | bytes 262176 | tf_op jit(solution)/shard_map/while/body/eval_jaxpr/ppermute | solution.py:19
  150.5 7.9 %collective-permute-done = f32[4,128,128]{2,1,0:T(8,128)S(1)} collective-permute-done((f32[4,128,128]{2,1,0:T(8,128)S(1)}, f32[4,128,128]{2,1,0:T(8,128)S(1)}, u32[]{:S(2)}, u32[]{:S(2)}) %collective-permute-start) | collective-permute-done | bytes 262176 | tf_op jit(solution)/shard_map/while/body/eval_jaxpr/ppermute | solution.py:19
  160.4 7.9 %collective-permute-done = f32[4,128,128]{2,1,0:T(8,128)S(1)} collective-permute-done((f32[4,128,128]{2,1,0:T(8,128)S(1)}, f32[4,128,128]{2,1,0:T(8,128)S(1)}, u32[]{:S(2)}, u32[]{:S(2)}) %collective-permute-start) | collective-permute-done | bytes 262176 | tf_op jit(solution)/shard_map/while/body/eval_jaxpr/ppermute | solution.py:19
  170.3 7.9 %collective-permute-done = f32[4,128,128]{2,1,0:T(8,128)S(1)} collective-permute-done((f32[4,128,128]{2,1,0:T(8,128)S(1)}, f32[4,128,128]{2,1,0:T(8,128)S(1)}, u32[]{:S(2)}, u32[]{:S(2)}) %collective-permute-start) | collective-permute-done | bytes 262176 | tf_op jit(solution)/shard_map/while/body/eval_jaxpr/ppermute | solution.py:19
  180.2 7.9 %collective-permute-done = f32[4,128,128]{2,1,0:T(8,128)S(1)} collective-permute-done((f32[4,128,128]{2,1,0:T(8,128)S(1)}, f32[4,128,128]{2,1,0:T(8,128)S(1)}, u32[]{:S(2)}, u32[]{:S(2)}) %collective-permute-start) | collective-permute-done | bytes 262176 | tf_op jit(solution)/shard_map/while/body/eval_jaxpr/ppermute | solution.py:19
  190.1 7.9 %collective-permute-done = f32[4,128,128]{2,1,0:T(8,128)S(1)} collective-permute-done((f32[4,128,128]{2,1,0:T(8,128)S(1)}, f32[4,128,128]{2,1,0:T(8,128)S(1)}, u32[]{:S(2)}, u32[]{:S(2)}) %collective-permute-start) | collective-permute-done | bytes 262176 | tf_op jit(solution)/shard_map/while/body/eval_jaxpr/ppermute | solution.py:19
  200.0 7.9 %collective-permute-done = f32[4,128,128]{2,1,0:T(8,128)S(1)} collective-permute-done((f32[4,128,128]{2,1,0:T(8,128)S(1)}, f32[4,128,128]{2,1,0:T(8,128)S(1)}, u32[]{:S(2)}, u32[]{:S(2)}) %collective-permute-start) | collective-permute-done | bytes 262176 | tf_op jit(solution)/shard_map/while/body/eval_jaxpr/ppermute | solution.py:19
  209.9 7.9 %collective-permute-done = f32[4,128,128]{2,1,0:T(8,128)S(1)} collective-permute-done((f32[4,128,128]{2,1,0:T(8,128)S(1)}, f32[4,128,128]{2,1,0:T(8,128)S(1)}, u32[]{:S(2)}, u32[]{:S(2)}) %collective-permute-start) | collective-permute-done | bytes 262176 | tf_op jit(solution)/shard_map/while/body/eval_jaxpr/ppermute | solution.py:19
  219.8 7.9 %collective-permute-done = f32[4,128,128]{2,1,0:T(8,128)S(1)} collective-permute-done((f32[4,128,128]{2,1,0:T(8,128)S(1)}, f32[4,128,128]{2,1,0:T(8,128)S(1)}, u32[]{:S(2)}, u32[]{:S(2)}) %collective-permute-start) | collective-permute-done | bytes 262176 | tf_op jit(solution)/shard_map/while/body/eval_jaxpr/ppermute | solution.py:19
  229.7 7.9 %collective-permute-done = f32[4,128,128]{2,1,0:T(8,128)S(1)} collective-permute-done((f32[4,128,128]{2,1,0:T(8,128)S(1)}, f32[4,128,128]{2,1,0:T(8,128)S(1)}, u32[]{:S(2)}, u32[]{:S(2)}) %collective-permute-start) | collective-permute-done | bytes 262176 | tf_op jit(solution)/shard_map/while/body/eval_jaxpr/ppermute | solution.py:19
  239.6 7.9 %collective-permute-done = f32[4,128,128]{2,1,0:T(8,128)S(1)} collective-permute-done((f32[4,128,128]{2,1,0:T(8,128)S(1)}, f32[4,128,128]{2,1,0:T(8,128)S(1)}, u32[]{:S(2)}, u32[]{:S(2)}) %collective-permute-start) | collective-permute-done | bytes 262176 | tf_op jit(solution)/shard_map/while/body/eval_jaxpr/ppermute | solution.py:19
  249.5 7.9 %collective-permute-done = f32[4,128,128]{2,1,0:T(8,128)S(1)} collective-permute-done((f32[4,128,128]{2,1,0:T(8,128)S(1)}, f32[4,128,128]{2,1,0:T(8,128)S(1)}, u32[]{:S(2)}, u32[]{:S(2)}) %collective-permute-start) | collective-permute-done | bytes 262176 | tf_op jit(solution)/shard_map/while/body/eval_jaxpr/ppermute | solution.py:19
  259.4 7.9 %collective-permute-done = f32[4,128,128]{2,1,0:T(8,128)S(1)} collective-permute-done((f32[4,128,128]{2,1,0:T(8,128)S(1)}, f32[4,128,128]{2,1,0:T(8,128)S(1)}, u32[]{:S(2)}, u32[]{:S(2)}) %collective-permute-start) | collective-permute-done | bytes 262176 | tf_op jit(solution)/shard_map/while/body/eval_jaxpr/ppermute | solution.py:19
  269.3 7.9 %collective-permute-done = f32[4,128,128]{2,1,0:T(8,128)S(1)} collective-permute-done((f32[4,128,128]{2,1,0:T(8,128)S(1)}, f32[4,128,128]{2,1,0:T(8,128)S(1)}, u32[]{:S(2)}, u32[]{:S(2)}) %collective-permute-start) | collective-permute-done | bytes 262176 | tf_op jit(solution)/shard_map/while/body/eval_jaxpr/ppermute | solution.py:19
  279.2 7.9 %collective-permute-done = f32[4,128,128]{2,1,0:T(8,128)S(1)} collective-permute-done((f32[4,128,128]{2,1,0:T(8,128)S(1)}, f32[4,128,128]{2,1,0:T(8,128)S(1)}, u32[]{:S(2)}, u32[]{:S(2)}) %collective-permute-start) | collective-permute-done | bytes 262176 | tf_op jit(solution)/shard_map/while/body/eval_jaxpr/ppermute | solution.py:19
  289.1 7.9 %collective-permute-done = f32[4,128,128]{2,1,0:T(8,128)S(1)} collective-permute-done((f32[4,128,128]{2,1,0:T(8,128)S(1)}, f32[4,128,128]{2,1,0:T(8,128)S(1)}, u32[]{:S(2)}, u32[]{:S(2)}) %collective-permute-start) | collective-permute-done | bytes 262176 | tf_op jit(solution)/shard_map/while/body/eval_jaxpr/ppermute | solution.py:19
  299.0 7.9 %collective-permute-done = f32[4,128,128]{2,1,0:T(8,128)S(1)} collective-permute-done((f32[4,128,128]{2,1,0:T(8,128)S(1)}, f32[4,128,128]{2,1,0:T(8,128)S(1)}, u32[]{:S(2)}, u32[]{:S(2)}) %collective-permute-start) | collective-permute-done | bytes 262176 | tf_op jit(solution)/shard_map/while/body/eval_jaxpr/ppermute | solution.py:19
  308.9 7.9 %collective-permute-done = f32[4,128,128]{2,1,0:T(8,128)S(1)} collective-permute-done((f32[4,128,128]{2,1,0:T(8,128)S(1)}, f32[4,128,128]{2,1,0:T(8,128)S(1)}, u32[]{:S(2)}, u32[]{:S(2)}) %collective-permute-start) | collective-permute-done | bytes 262176 | tf_op jit(solution)/shard_map/while/body/eval_jaxpr/ppermute | solution.py:19
  318.8 7.9 %collective-permute-done = f32[4,128,128]{2,1,0:T(8,128)S(1)} collective-permute-done((f32[4,128,128]{2,1,0:T(8,128)S(1)}, f32[4,128,128]{2,1,0:T(8,128)S(1)}, u32[]{:S(2)}, u32[]{:S(2)}) %collective-permute-start) | collective-permute-done | bytes 262176 | tf_op jit(solution)/shard_map/while/body/eval_jaxpr/ppermute | solution.py:19
  328.2 37.5 %psum.7 = f32[256]{0:T(256)S(1)} all-reduce(f32[256]{0:T(256)S(1)} %get-tuple-element.439), channel_id=1, replica_groups=mesh['ctx'=32,'head'=16] {'head'}, use_global_device_ids=true, to_apply=%region_5.6 | all-reduce | flops 256 | bytes 2048 | tf_op jit(solution)/shard_map/psum | solution.py:117
  366.6 76.8 %while.36 = (s32[]{:T(128)}, f32[4,256]{1,0:T(4,128)S(1)}, f32[4,256]{1,0:T(4,128)S(1)}, f32[4,256,128]{2,1,0:T(8,128)S(1)}, s32[]{:T(128)}, /*index=5*/bf16[819...) while((s32[]{:T(128)}, f32[4,256]{1,0:T(4,128)S(1)}, ...), condition=%wide.region_11.12_spmd.clone, body=%wide.region_6.11_spmd.clone.sunk | while | flops 137431552 | bytes 4922689 | solution.py:76
  366.6 3.0 conditional.3
  369.7 3.0 conditional.3
  375.8 3.0 conditional.3
  378.8 3.0 conditional.3
  384.9 3.0 conditional.3
  388.0 3.0 conditional.3
  394.1 3.0 conditional.3
  397.2 3.0 conditional.3
  403.3 3.0 conditional.3
  406.3 3.0 conditional.3
  412.5 3.0 conditional.3
  415.5 3.0 conditional.3
  424.7 3.0 conditional.3
  433.9 3.0 conditional.3
  (356 shorter events, 181.9 us)
Async XLA Ops:
  7.2 1.0 copy-start
  7.2 8.2 %copy-start.1 = (bf16[256,512]{1,0:T(8,128)(2,1)S(1)}, bf16[256,512]{1,0:T(8,128)(2,1)}, u32[]{:S(2)}) copy-start(bf16[256,512]{1,0:T(8,128)(2,1)} %param.14) | copy-start | bytes 786436
  7.2 9.0 %copy-start.2 = (bf16[256,512]{1,0:T(8,128)(2,1)S(1)}, bf16[256,512]{1,0:T(8,128)(2,1)}, u32[]{:S(2)}) copy-start(bf16[256,512]{1,0:T(8,128)(2,1)} %param.16) | copy-start | bytes 786436
  7.2 359.3 %all-gather.3.cloned.1.call-start = ((), (), s32[]{:S(2)}) async-start(), calls=%async_computation | async-start | bytes 2162688 | tf_op jit(solution)/shard_map/all_gather | solution.py:158
  8.9 357.6 %all-gather.5.cloned.1.call-start = ((), (), s32[]{:S(2)}) async-start(), calls=%async_computation.1 | async-start | bytes 2162688 | tf_op jit(solution)/shard_map/all_gather | solution.py:159
  16.5 9.8 %collective-permute-start = (f32[4,128,128]{2,1,0:T(8,128)S(1)}, f32[4,128,128]{2,1,0:T(8,128)S(1)}, u32[]{:S(2)}, u32[]{:S(2)}) collective-permute-start(f32[4,128,128]{2,1,0:T(8,128)S(1)} %multiply_add_fusion.3), channel_id=1, source_target_pairs={{0,16},{16,32},{32,48},{48,64},{64,80},{80,96},{96,112},{112,128},... | collective-permute-start | bytes 786440 | tf_op jit(solution)/shard_map/while/body/eval_jaxpr/ppermute | solution.py:19
  26.4 9.8 %collective-permute-start = (f32[4,128,128]{2,1,0:T(8,128)S(1)}, f32[4,128,128]{2,1,0:T(8,128)S(1)}, u32[]{:S(2)}, u32[]{:S(2)}) collective-permute-start(f32[4,128,128]{2,1,0:T(8,128)S(1)} %multiply_add_fusion.3), channel_id=1, source_target_pairs={{0,16},{16,32},{32,48},{48,64},{64,80},{80,96},{96,112},{112,128},... | collective-permute-start | bytes 786440 | tf_op jit(solution)/shard_map/while/body/eval_jaxpr/ppermute | solution.py:19
  36.3 10.0 %collective-permute-start = (f32[4,128,128]{2,1,0:T(8,128)S(1)}, f32[4,128,128]{2,1,0:T(8,128)S(1)}, u32[]{:S(2)}, u32[]{:S(2)}) collective-permute-start(f32[4,128,128]{2,1,0:T(8,128)S(1)} %multiply_add_fusion.3), channel_id=1, source_target_pairs={{0,16},{16,32},{32,48},{48,64},{64,80},{80,96},{96,112},{112,128},... | collective-permute-start | bytes 786440 | tf_op jit(solution)/shard_map/while/body/eval_jaxpr/ppermute | solution.py:19
  46.4 9.8 %collective-permute-start = (f32[4,128,128]{2,1,0:T(8,128)S(1)}, f32[4,128,128]{2,1,0:T(8,128)S(1)}, u32[]{:S(2)}, u32[]{:S(2)}) collective-permute-start(f32[4,128,128]{2,1,0:T(8,128)S(1)} %multiply_add_fusion.3), channel_id=1, source_target_pairs={{0,16},{16,32},{32,48},{48,64},{64,80},{80,96},{96,112},{112,128},... | collective-permute-start | bytes 786440 | tf_op jit(solution)/shard_map/while/body/eval_jaxpr/ppermute | solution.py:19
  56.3 10.3 %collective-permute-start = (f32[4,128,128]{2,1,0:T(8,128)S(1)}, f32[4,128,128]{2,1,0:T(8,128)S(1)}, u32[]{:S(2)}, u32[]{:S(2)}) collective-permute-start(f32[4,128,128]{2,1,0:T(8,128)S(1)} %multiply_add_fusion.3), channel_id=1, source_target_pairs={{0,16},{16,32},{32,48},{48,64},{64,80},{80,96},{96,112},{112,128},... | collective-permute-start | bytes 786440 | tf_op jit(solution)/shard_map/while/body/eval_jaxpr/ppermute | solution.py:19
  66.7 10.7 %collective-permute-start = (f32[4,128,128]{2,1,0:T(8,128)S(1)}, f32[4,128,128]{2,1,0:T(8,128)S(1)}, u32[]{:S(2)}, u32[]{:S(2)}) collective-permute-start(f32[4,128,128]{2,1,0:T(8,128)S(1)} %multiply_add_fusion.3), channel_id=1, source_target_pairs={{0,16},{16,32},{32,48},{48,64},{64,80},{80,96},{96,112},{112,128},... | collective-permute-start | bytes 786440 | tf_op jit(solution)/shard_map/while/body/eval_jaxpr/ppermute | solution.py:19
  77.5 9.8 %collective-permute-start = (f32[4,128,128]{2,1,0:T(8,128)S(1)}, f32[4,128,128]{2,1,0:T(8,128)S(1)}, u32[]{:S(2)}, u32[]{:S(2)}) collective-permute-start(f32[4,128,128]{2,1,0:T(8,128)S(1)} %multiply_add_fusion.3), channel_id=1, source_target_pairs={{0,16},{16,32},{32,48},{48,64},{64,80},{80,96},{96,112},{112,128},... | collective-permute-start | bytes 786440 | tf_op jit(solution)/shard_map/while/body/eval_jaxpr/ppermute | solution.py:19
  87.4 9.8 %collective-permute-start = (f32[4,128,128]{2,1,0:T(8,128)S(1)}, f32[4,128,128]{2,1,0:T(8,128)S(1)}, u32[]{:S(2)}, u32[]{:S(2)}) collective-permute-start(f32[4,128,128]{2,1,0:T(8,128)S(1)} %multiply_add_fusion.3), channel_id=1, source_target_pairs={{0,16},{16,32},{32,48},{48,64},{64,80},{80,96},{96,112},{112,128},... | collective-permute-start | bytes 786440 | tf_op jit(solution)/shard_map/while/body/eval_jaxpr/ppermute | solution.py:19
  97.3 10.2 %collective-permute-start = (f32[4,128,128]{2,1,0:T(8,128)S(1)}, f32[4,128,128]{2,1,0:T(8,128)S(1)}, u32[]{:S(2)}, u32[]{:S(2)}) collective-permute-start(f32[4,128,128]{2,1,0:T(8,128)S(1)} %multiply_add_fusion.3), channel_id=1, source_target_pairs={{0,16},{16,32},{32,48},{48,64},{64,80},{80,96},{96,112},{112,128},... | collective-permute-start | bytes 786440 | tf_op jit(solution)/shard_map/while/body/eval_jaxpr/ppermute | solution.py:19
  107.6 9.8 %collective-permute-start = (f32[4,128,128]{2,1,0:T(8,128)S(1)}, f32[4,128,128]{2,1,0:T(8,128)S(1)}, u32[]{:S(2)}, u32[]{:S(2)}) collective-permute-start(f32[4,128,128]{2,1,0:T(8,128)S(1)} %multiply_add_fusion.3), channel_id=1, source_target_pairs={{0,16},{16,32},{32,48},{48,64},{64,80},{80,96},{96,112},{112,128},... | collective-permute-start | bytes 786440 | tf_op jit(solution)/shard_map/while/body/eval_jaxpr/ppermute | solution.py:19
  117.5 9.8 %collective-permute-start = (f32[4,128,128]{2,1,0:T(8,128)S(1)}, f32[4,128,128]{2,1,0:T(8,128)S(1)}, u32[]{:S(2)}, u32[]{:S(2)}) collective-permute-start(f32[4,128,128]{2,1,0:T(8,128)S(1)} %multiply_add_fusion.3), channel_id=1, source_target_pairs={{0,16},{16,32},{32,48},{48,64},{64,80},{80,96},{96,112},{112,128},... | collective-permute-start | bytes 786440 | tf_op jit(solution)/shard_map/while/body/eval_jaxpr/ppermute | solution.py:19
  127.4 11.2 %collective-permute-start = (f32[4,128,128]{2,1,0:T(8,128)S(1)}, f32[4,128,128]{2,1,0:T(8,128)S(1)}, u32[]{:S(2)}, u32[]{:S(2)}) collective-permute-start(f32[4,128,128]{2,1,0:T(8,128)S(1)} %multiply_add_fusion.3), channel_id=1, source_target_pairs={{0,16},{16,32},{32,48},{48,64},{64,80},{80,96},{96,112},{112,128},... | collective-permute-start | bytes 786440 | tf_op jit(solution)/shard_map/while/body/eval_jaxpr/ppermute | solution.py:19
  138.7 9.8 %collective-permute-start = (f32[4,128,128]{2,1,0:T(8,128)S(1)}, f32[4,128,128]{2,1,0:T(8,128)S(1)}, u32[]{:S(2)}, u32[]{:S(2)}) collective-permute-start(f32[4,128,128]{2,1,0:T(8,128)S(1)} %multiply_add_fusion.3), channel_id=1, source_target_pairs={{0,16},{16,32},{32,48},{48,64},{64,80},{80,96},{96,112},{112,128},... | collective-permute-start | bytes 786440 | tf_op jit(solution)/shard_map/while/body/eval_jaxpr/ppermute | solution.py:19
  148.6 9.8 %collective-permute-start = (f32[4,128,128]{2,1,0:T(8,128)S(1)}, f32[4,128,128]{2,1,0:T(8,128)S(1)}, u32[]{:S(2)}, u32[]{:S(2)}) collective-permute-start(f32[4,128,128]{2,1,0:T(8,128)S(1)} %multiply_add_fusion.3), channel_id=1, source_target_pairs={{0,16},{16,32},{32,48},{48,64},{64,80},{80,96},{96,112},{112,128},... | collective-permute-start | bytes 786440 | tf_op jit(solution)/shard_map/while/body/eval_jaxpr/ppermute | solution.py:19
  158.5 9.8 %collective-permute-start = (f32[4,128,128]{2,1,0:T(8,128)S(1)}, f32[4,128,128]{2,1,0:T(8,128)S(1)}, u32[]{:S(2)}, u32[]{:S(2)}) collective-permute-start(f32[4,128,128]{2,1,0:T(8,128)S(1)} %multiply_add_fusion.3), channel_id=1, source_target_pairs={{0,16},{16,32},{32,48},{48,64},{64,80},{80,96},{96,112},{112,128},... | collective-permute-start | bytes 786440 | tf_op jit(solution)/shard_map/while/body/eval_jaxpr/ppermute | solution.py:19
  168.4 9.8 %collective-permute-start = (f32[4,128,128]{2,1,0:T(8,128)S(1)}, f32[4,128,128]{2,1,0:T(8,128)S(1)}, u32[]{:S(2)}, u32[]{:S(2)}) collective-permute-start(f32[4,128,128]{2,1,0:T(8,128)S(1)} %multiply_add_fusion.3), channel_id=1, source_target_pairs={{0,16},{16,32},{32,48},{48,64},{64,80},{80,96},{96,112},{112,128},... | collective-permute-start | bytes 786440 | tf_op jit(solution)/shard_map/while/body/eval_jaxpr/ppermute | solution.py:19
  178.3 9.8 %collective-permute-start = (f32[4,128,128]{2,1,0:T(8,128)S(1)}, f32[4,128,128]{2,1,0:T(8,128)S(1)}, u32[]{:S(2)}, u32[]{:S(2)}) collective-permute-start(f32[4,128,128]{2,1,0:T(8,128)S(1)} %multiply_add_fusion.3), channel_id=1, source_target_pairs={{0,16},{16,32},{32,48},{48,64},{64,80},{80,96},{96,112},{112,128},... | collective-permute-start | bytes 786440 | tf_op jit(solution)/shard_map/while/body/eval_jaxpr/ppermute | solution.py:19
  188.2 9.8 %collective-permute-start = (f32[4,128,128]{2,1,0:T(8,128)S(1)}, f32[4,128,128]{2,1,0:T(8,128)S(1)}, u32[]{:S(2)}, u32[]{:S(2)}) collective-permute-start(f32[4,128,128]{2,1,0:T(8,128)S(1)} %multiply_add_fusion.3), channel_id=1, source_target_pairs={{0,16},{16,32},{32,48},{48,64},{64,80},{80,96},{96,112},{112,128},... | collective-permute-start | bytes 786440 | tf_op jit(solution)/shard_map/while/body/eval_jaxpr/ppermute | solution.py:19
  198.1 9.8 %collective-permute-start = (f32[4,128,128]{2,1,0:T(8,128)S(1)}, f32[4,128,128]{2,1,0:T(8,128)S(1)}, u32[]{:S(2)}, u32[]{:S(2)}) collective-permute-start(f32[4,128,128]{2,1,0:T(8,128)S(1)} %multiply_add_fusion.3), channel_id=1, source_target_pairs={{0,16},{16,32},{32,48},{48,64},{64,80},{80,96},{96,112},{112,128},... | collective-permute-start | bytes 786440 | tf_op jit(solution)/shard_map/while/body/eval_jaxpr/ppermute | solution.py:19
  208.0 9.8 %collective-permute-start = (f32[4,128,128]{2,1,0:T(8,128)S(1)}, f32[4,128,128]{2,1,0:T(8,128)S(1)}, u32[]{:S(2)}, u32[]{:S(2)}) collective-permute-start(f32[4,128,128]{2,1,0:T(8,128)S(1)} %multiply_add_fusion.3), channel_id=1, source_target_pairs={{0,16},{16,32},{32,48},{48,64},{64,80},{80,96},{96,112},{112,128},... | collective-permute-start | bytes 786440 | tf_op jit(solution)/shard_map/while/body/eval_jaxpr/ppermute | solution.py:19
  217.9 9.8 %collective-permute-start = (f32[4,128,128]{2,1,0:T(8,128)S(1)}, f32[4,128,128]{2,1,0:T(8,128)S(1)}, u32[]{:S(2)}, u32[]{:S(2)}) collective-permute-start(f32[4,128,128]{2,1,0:T(8,128)S(1)} %multiply_add_fusion.3), channel_id=1, source_target_pairs={{0,16},{16,32},{32,48},{48,64},{64,80},{80,96},{96,112},{112,128},... | collective-permute-start | bytes 786440 | tf_op jit(solution)/shard_map/while/body/eval_jaxpr/ppermute | solution.py:19
  227.8 9.8 %collective-permute-start = (f32[4,128,128]{2,1,0:T(8,128)S(1)}, f32[4,128,128]{2,1,0:T(8,128)S(1)}, u32[]{:S(2)}, u32[]{:S(2)}) collective-permute-start(f32[4,128,128]{2,1,0:T(8,128)S(1)} %multiply_add_fusion.3), channel_id=1, source_target_pairs={{0,16},{16,32},{32,48},{48,64},{64,80},{80,96},{96,112},{112,128},... | collective-permute-start | bytes 786440 | tf_op jit(solution)/shard_map/while/body/eval_jaxpr/ppermute | solution.py:19
  237.7 9.8 %collective-permute-start = (f32[4,128,128]{2,1,0:T(8,128)S(1)}, f32[4,128,128]{2,1,0:T(8,128)S(1)}, u32[]{:S(2)}, u32[]{:S(2)}) collective-permute-start(f32[4,128,128]{2,1,0:T(8,128)S(1)} %multiply_add_fusion.3), channel_id=1, source_target_pairs={{0,16},{16,32},{32,48},{48,64},{64,80},{80,96},{96,112},{112,128},... | collective-permute-start | bytes 786440 | tf_op jit(solution)/shard_map/while/body/eval_jaxpr/ppermute | solution.py:19
  247.5 9.8 %collective-permute-start = (f32[4,128,128]{2,1,0:T(8,128)S(1)}, f32[4,128,128]{2,1,0:T(8,128)S(1)}, u32[]{:S(2)}, u32[]{:S(2)}) collective-permute-start(f32[4,128,128]{2,1,0:T(8,128)S(1)} %multiply_add_fusion.3), channel_id=1, source_target_pairs={{0,16},{16,32},{32,48},{48,64},{64,80},{80,96},{96,112},{112,128},... | collective-permute-start | bytes 786440 | tf_op jit(solution)/shard_map/while/body/eval_jaxpr/ppermute | solution.py:19
  257.4 9.8 %collective-permute-start = (f32[4,128,128]{2,1,0:T(8,128)S(1)}, f32[4,128,128]{2,1,0:T(8,128)S(1)}, u32[]{:S(2)}, u32[]{:S(2)}) collective-permute-start(f32[4,128,128]{2,1,0:T(8,128)S(1)} %multiply_add_fusion.3), channel_id=1, source_target_pairs={{0,16},{16,32},{32,48},{48,64},{64,80},{80,96},{96,112},{112,128},... | collective-permute-start | bytes 786440 | tf_op jit(solution)/shard_map/while/body/eval_jaxpr/ppermute | solution.py:19
  267.3 9.8 %collective-permute-start = (f32[4,128,128]{2,1,0:T(8,128)S(1)}, f32[4,128,128]{2,1,0:T(8,128)S(1)}, u32[]{:S(2)}, u32[]{:S(2)}) collective-permute-start(f32[4,128,128]{2,1,0:T(8,128)S(1)} %multiply_add_fusion.3), channel_id=1, source_target_pairs={{0,16},{16,32},{32,48},{48,64},{64,80},{80,96},{96,112},{112,128},... | collective-permute-start | bytes 786440 | tf_op jit(solution)/shard_map/while/body/eval_jaxpr/ppermute | solution.py:19
  277.2 9.8 %collective-permute-start = (f32[4,128,128]{2,1,0:T(8,128)S(1)}, f32[4,128,128]{2,1,0:T(8,128)S(1)}, u32[]{:S(2)}, u32[]{:S(2)}) collective-permute-start(f32[4,128,128]{2,1,0:T(8,128)S(1)} %multiply_add_fusion.3), channel_id=1, source_target_pairs={{0,16},{16,32},{32,48},{48,64},{64,80},{80,96},{96,112},{112,128},... | collective-permute-start | bytes 786440 | tf_op jit(solution)/shard_map/while/body/eval_jaxpr/ppermute | solution.py:19
  287.1 9.8 %collective-permute-start = (f32[4,128,128]{2,1,0:T(8,128)S(1)}, f32[4,128,128]{2,1,0:T(8,128)S(1)}, u32[]{:S(2)}, u32[]{:S(2)}) collective-permute-start(f32[4,128,128]{2,1,0:T(8,128)S(1)} %multiply_add_fusion.3), channel_id=1, source_target_pairs={{0,16},{16,32},{32,48},{48,64},{64,80},{80,96},{96,112},{112,128},... | collective-permute-start | bytes 786440 | tf_op jit(solution)/shard_map/while/body/eval_jaxpr/ppermute | solution.py:19
  297.0 9.8 %collective-permute-start = (f32[4,128,128]{2,1,0:T(8,128)S(1)}, f32[4,128,128]{2,1,0:T(8,128)S(1)}, u32[]{:S(2)}, u32[]{:S(2)}) collective-permute-start(f32[4,128,128]{2,1,0:T(8,128)S(1)} %multiply_add_fusion.3), channel_id=1, source_target_pairs={{0,16},{16,32},{32,48},{48,64},{64,80},{80,96},{96,112},{112,128},... | collective-permute-start | bytes 786440 | tf_op jit(solution)/shard_map/while/body/eval_jaxpr/ppermute | solution.py:19
  306.9 9.8 %collective-permute-start = (f32[4,128,128]{2,1,0:T(8,128)S(1)}, f32[4,128,128]{2,1,0:T(8,128)S(1)}, u32[]{:S(2)}, u32[]{:S(2)}) collective-permute-start(f32[4,128,128]{2,1,0:T(8,128)S(1)} %multiply_add_fusion.3), channel_id=1, source_target_pairs={{0,16},{16,32},{32,48},{48,64},{64,80},{80,96},{96,112},{112,128},... | collective-permute-start | bytes 786440 | tf_op jit(solution)/shard_map/while/body/eval_jaxpr/ppermute | solution.py:19
  316.8 9.8 %collective-permute-start = (f32[4,128,128]{2,1,0:T(8,128)S(1)}, f32[4,128,128]{2,1,0:T(8,128)S(1)}, u32[]{:S(2)}, u32[]{:S(2)}) collective-permute-start(f32[4,128,128]{2,1,0:T(8,128)S(1)} %multiply_add_fusion.3), channel_id=1, source_target_pairs={{0,16},{16,32},{32,48},{48,64},{64,80},{80,96},{96,112},{112,128},... | collective-permute-start | bytes 786440 | tf_op jit(solution)/shard_map/while/body/eval_jaxpr/ppermute | solution.py:19
  327.4 38.3 %copy-start.3 = (f32[512]{0:T(512)S(1)}, f32[512]{0:T(512)}, u32[]{:S(2)}) copy-start(f32[512]{0:T(512)} %param.18) | copy-start | bytes 6148
Sparse Core Ops, SparseCore 0:
  11.7 64.7 all-gather.2
  79.7 60.1 all-gather.4
where the time goes:
time: 455 us; the launch traced here: 451 us
  waiting for transfers between devices  247 us (54%)
  matrix products  66.5 us (15%)
  starting transfers between devices  59.6 us (13%)
  blocking collectives  37.5 us (8%)
  other arithmetic  15.5 us (3%)
  between operations  14.2 us (3%)
  local copies, waits for them, and re-layouts  7.01 us (2%)
    ppermute x31, waiting for transfers between devices, shifted(): lax.ppermute(value, axis, [(source, source + steps) for source in range(f...  247 us
    ppermute x31, starting transfers between devices, shifted(): lax.ppermute(value, axis, [(source, source + steps) for source in range(f...  59.5 us
    psum x1, blocking collectives, local(): lax.psum(jnp.sum(mixed * mixed, axis=1), 'head') / (QUERY_HEADS * DH)  37.5 us
    dot_general x25, matrix products, soft_update(): jnp.einsum('kgts,ske->kgte', rounded, value_rows, preferred_element_type=...  35 us
    dot_general x25, matrix products, soft_update(): jnp.einsum('tkgd,skd->kgts', queries, key_rows, preferred_element_type=jn...  29.2 us
  transfers between devices with their start and end apart: 33, of which 31 were waited for; matrix products, arithmetic and copies ran while one was open for 3% of the time, Pallas kernels for 0%

commit v1 on v0

v1 whole, which is shorter than its diff:
```python
import functools

import jax
import jax.numpy as jnp
from jax import lax
from jax.experimental import pallas as pl
from jax.experimental.pallas import tpu as pltpu
from jax.sharding import PartitionSpec as P

QUERY_HEADS = 64
DH = 128
KV_HEADS = 8
BLOCK = 256
KEY_BLOCK = 256


EPSILON = 1e-06
NEGATIVE = -1e30


def shifted(value, axis, steps):
    count = lax.axis_size(axis)
    first, last = (max(0, -steps), min(count, count - steps))
    return lax.ppermute(value, axis, [(source, source + steps) for source in range(first, last)])


def lightning_step(carry, inputs):
    running, log_before = carry
    queries, key_rows, value_rows, log_gates = inputs
    row_count = queries.shape[0]
    cumulative = jnp.cumsum(log_gates, axis=0)
    final_log = cumulative[-1]
    positions = jnp.arange(row_count, dtype=jnp.int32)
    causal = positions[None, :] <= positions[:, None]
    cum_heads = cumulative.T
    log_gap = jnp.where(causal[None], cum_heads[:, :, None] - cum_heads[:, None, :], NEGATIVE)
    scores = jnp.einsum("thd,shd->hts", queries, key_rows, preferred_element_type=jnp.float32)
    weights = (scores * jnp.exp(log_gap)).astype(jnp.bfloat16)
    intra_part = jnp.einsum("hts,she->the", weights, value_rows, preferred_element_type=jnp.float32)
    query_wide = queries.astype(jnp.float32)
    lifted_here = query_wide * jnp.exp(cumulative)[:, :, None]
    carried_here = jnp.einsum("thd,hde->the", lifted_here, running, precision=lax.Precision.HIGHEST)
    lifted_device = query_wide * jnp.exp(cumulative + log_before[None, :])[:, :, None]
    scaled = (key_rows * jnp.exp(final_log[None, :] - cumulative)[:, :, None]).astype(jnp.bfloat16)
    block_state = jnp.einsum("shd,she->hde", scaled, value_rows, preferred_element_type=jnp.float32)
    running = jnp.exp(final_log)[:, None, None] * running + block_state
    return ((running, log_before + final_log), (intra_part + carried_here, lifted_device))


def exclusive_scan(log_total, block_state, axis):
    log_acc, state_acc = shifted((log_total, block_state), axis, 1)
    count = lax.axis_size(axis)
    step = 1
    while step < count:
        log_in, state_in = shifted((log_acc, state_acc), axis, step)
        state_acc = jnp.exp(log_acc)[:, None, None] * state_in + state_acc
        log_acc = log_acc + log_in
        step *= 2
    return state_acc


def soft_kernel(index_ref, q_ref, kv_ref, o_ref, max_ref, total_ref, acc_ref):
    my_index = index_ref[0]
    row_count = q_ref.shape[0]
    head_count = q_ref.shape[1] // DH
    max_ref[...] = jnp.full(max_ref.shape, NEGATIVE, jnp.float32)
    total_ref[...] = jnp.zeros(total_ref.shape, jnp.float32)
    acc_ref[...] = jnp.zeros(acc_ref.shape, jnp.float32)
    query_pos = my_index * row_count + lax.broadcasted_iota(jnp.int32, (row_count, KEY_BLOCK), 0)
    block_count = (my_index * row_count + row_count - 1) // KEY_BLOCK + 1

    def body(block, carry):
        start = pl.multiple_of(block * KEY_BLOCK, KEY_BLOCK)
        keys = kv_ref[pl.ds(start, KEY_BLOCK), 0:DH]
        values = kv_ref[pl.ds(start, KEY_BLOCK), DH : 2 * DH]
        key_pos = start + lax.broadcasted_iota(jnp.int32, (row_count, KEY_BLOCK), 1)
        allowed = key_pos <= query_pos
        for head in range(head_count):
            queries = q_ref[:, head * DH : (head + 1) * DH]
            scores = lax.dot_general(
                queries, keys, (((1,), (1,)), ((), ())), preferred_element_type=jnp.float32
            ) * DH ** (-0.5)
            scores = jnp.where(allowed, scores, NEGATIVE)
            row_max = max_ref[head]
            new_max = jnp.maximum(row_max, jnp.max(scores, axis=1, keepdims=True))
            probabilities = jnp.where(allowed, jnp.exp(scores - new_max), 0.0)
            rescale = jnp.exp(row_max - new_max)
            total_ref[head] = total_ref[head] * rescale + jnp.sum(probabilities, axis=1, keepdims=True)
            product = jnp.dot(
                probabilities.astype(jnp.bfloat16), values, preferred_element_type=jnp.float32
            )
            acc_ref[head] = acc_ref[head] * rescale + product
            max_ref[head] = new_max
        return carry

    lax.fori_loop(0, block_count, body, 0)
    for head in range(head_count):
        o_ref[:, head * DH : (head + 1) * DH] = (acc_ref[head] / total_ref[head]).astype(o_ref.dtype)


def soft_attention(my_index, queries, keys_values):
    row_count, width = queries.shape
    head_count = width // DH
    return pl.pallas_call(
        soft_kernel,
        out_shape=jax.ShapeDtypeStruct((row_count, width), jnp.bfloat16),
        in_specs=[
            pl.BlockSpec(memory_space=pltpu.SMEM),
            pl.BlockSpec(memory_space=pltpu.VMEM),
            pl.BlockSpec(memory_space=pltpu.VMEM),
        ],
        out_specs=pl.BlockSpec(memory_space=pltpu.VMEM),
        scratch_shapes=[
            pltpu.VMEM((head_count, row_count, 1), jnp.float32),
            pltpu.VMEM((head_count, row_count, 1), jnp.float32),
            pltpu.VMEM((head_count, row_count, DH), jnp.float32),
        ],
    )(my_index.reshape(1), queries, keys_values)


def local(q_linear, k_linear, v_linear, log_decay, norm_gain, q_soft, k_soft, v_soft):
    row_count = q_linear.shape[0]
    head_count = log_decay.shape[1]
    width = head_count * DH
    group_size = QUERY_HEADS // KV_HEADS
    kv_count = max(1, head_count // group_size)
    kv_start = lax.axis_index("head") * head_count // group_size
    k_local = lax.dynamic_slice_in_dim(k_soft, kv_start * DH, kv_count * DH, 1)
    v_local = lax.dynamic_slice_in_dim(v_soft, kv_start * DH, kv_count * DH, 1)
    keys_values = lax.all_gather(
        jnp.concatenate([k_local, v_local], axis=1), "ctx", axis=0, tiled=True
    )

    local_blocks = row_count // BLOCK
    lin_shape = (local_blocks, BLOCK, head_count, DH)
    sequences = (
        q_linear.reshape(lin_shape),
        k_linear.reshape(lin_shape),
        v_linear.reshape(lin_shape),
        log_decay.reshape(local_blocks, BLOCK, head_count),
    )
    start_carry = (
        jnp.zeros((head_count, DH, DH), jnp.float32),
        jnp.zeros((head_count,), jnp.float32),
    )
    (block_state, log_total), (local_part, lifted) = lax.scan(
        lightning_step, start_carry, sequences
    )
    local_part = local_part.reshape(row_count, head_count, DH)
    lifted = lifted.reshape(row_count, head_count, DH)
    entering = exclusive_scan(log_total, block_state, "ctx")
    carried = jnp.einsum("thd,hde->the", lifted, entering, precision=lax.Precision.HIGHEST)
    mixed = (local_part + carried).reshape(row_count, width)
    power = lax.psum(jnp.sum(mixed * mixed, axis=1), "head") / (QUERY_HEADS * DH)
    linear_out = (mixed * lax.rsqrt(power + EPSILON)[:, None] * norm_gain[None, :]).astype(
        jnp.bfloat16
    )

    my_index = lax.axis_index("ctx").astype(jnp.int32)
    if kv_count == 1:
        soft_out = soft_attention(my_index, q_soft, keys_values)
    else:
        raise NotImplementedError("kv_count > 1")
    return (linear_out, soft_out)


def solution(mesh):
    return jax.shard_map(
        local,
        mesh=mesh,
        in_specs=(
            P("ctx", "head"),
            P("ctx", "head"),
            P("ctx", "head"),
            P("ctx", "head"),
            P("head"),
            P("ctx", "head"),
            P("ctx", None),
            P("ctx", None),
        ),
        out_specs=(P("ctx", "head"), P("ctx", "head")),
        check_vma=False,
    )
```

time: 455 us -> 206 us (0.45)
  the two profiles are of different devices: /device:TPU:6 before, /device:TPU:22 now
where the time goes in v1:
time: 206 us; the launch traced here: 205 us
  Pallas kernels  74.4 us (36%)
  waiting for transfers between devices  46 us (22%)
  blocking collectives  39.7 us (19%)
  starting transfers between devices  21.1 us (10%)
  between operations  14.3 us (7%)
  local copies, waits for them, and re-layouts  3.41 us (2%)
  other arithmetic  3.33 us (2%)
  matrix products  3.29 us (2%)
    pallas_call x1, Pallas kernels, soft_attention(): pl.pallas_call(soft_kernel, out_shape=jax.ShapeDtypeStruct((row_count, wi...  74.4 us
    ppermute x11, waiting for transfers between devices, shifted(): lax.ppermute(value, axis, [(source, source + steps) for source in range(f...  46 us
    psum x1, blocking collectives, local(): lax.psum(jnp.sum(mixed * mixed, axis=1), 'head') / (QUERY_HEADS * DH)  39.7 us
    ppermute x11, starting transfers between devices, shifted(): lax.ppermute(value, axis, [(source, source + steps) for source in range(f...  21 us
  transfers between devices with their start and end apart: 12, of which 10 were waited for; matrix products, arithmetic and copies ran while one was open for 4% of the time, Pallas kernels for 0%

profile of v1, /device:TPU:22, one launch (start us, length us, event | category | flops | bytes accessed | tf_op | source)
XLA Modules:
  0.0 205.5 jit_solution(10538871675142487359)
XLA Ops:
  7.2 0.0 copy-start
  7.2 0.0 copy-start.1
  7.2 0.0 all-gather.2.cloned.1.call-start
  7.3 0.9 constant_dynamic-slice_fusion
  8.2 0.7 pad_maximum_fusion
  8.9 0.0 all-gather.2.cloned.1.call-update
  8.9 0.7 reshape.82
  9.6 1.2 reduce-window.6
  10.8 0.1 slice.13
  10.9 0.1 copy.31
  11.0 0.1 copy.32
  11.1 0.1 add_bitcast_fusion
  11.2 1.1 copy.40
  12.3 0.2 slice_reduce_fusion
  12.5 0.1 subtract_exponential_fusion
  12.6 1.2 convolution_add_fusion
  13.7 1.9 collective-permute-start.5
  15.7 5.8 %collective-permute-done.5 = f32[4,128,128]{2,1,0:T(8,128)S(1)} collective-permute-done((f32[4,128,128]{2,1,0:T(8,128)S(1)}, f32[4,128,128]{2,1,0:T(8,128)S(1)}, u32[]{:S(2)}, u32[]{:S(2)}) %collective-permute-start.5) | collective-permute-done | bytes 262176 | tf_op jit(solution)/shard_map/ppermute | solution.py:24
  21.4 1.9 collective-permute-start.6
  23.4 3.3 %collective-permute-start = (f32[4]{0:T(128)S(1)}, f32[4]{0:T(128)S(1)}, u32[]{:S(2)}, u32[]{:S(2)}) collective-permute-start(f32[4]{0:T(128)S(1)} %slice_reduce_fusion), channel_id=1, source_target_pairs={{0,16},{16,32},{32,48},{48,64},{64,80},{80,96},{96,112},{112,128},... | collective-permute-start | bytes 56 | tf_op jit(solution)/shard_map/ppermute | solution.py:24
  26.7 2.6 %collective-permute-done = f32[4]{0:T(128)S(1)} collective-permute-done((f32[4]{0:T(128)S(1)}, f32[4]{0:T(128)S(1)}, u32[]{:S(2)}, u32[]{:S(2)}) %collective-permute-start) | collective-permute-done | bytes 48 | tf_op jit(solution)/shard_map/ppermute | solution.py:24
  29.2 1.9 collective-permute-start.1
  31.1 3.0 %collective-permute-done.1 = f32[4]{0:T(128)S(1)} collective-permute-done((f32[4]{0:T(128)S(1)}, f32[4]{0:T(128)S(1)}, u32[]{:S(2)}, u32[]{:S(2)}) %collective-permute-start.1) | collective-permute-done | bytes 48 | tf_op jit(solution)/shard_map/ppermute | solution.py:24
  34.1 0.1 multiply_add_fusion.3
  34.2 3.2 %collective-permute-start.7 = (f32[4,128,128]{2,1,0:T(8,128)S(1)}, f32[4,128,128]{2,1,0:T(8,128)S(1)}, u32[]{:S(2)}, u32[]{:S(2)}) collective-permute-start(f32[4,128,128]{2,1,0:T(8,128)S(1)} %multiply_add_fusion.3), channel_id=1, source_target_pairs={{0,32},{16,48},{32,64},{48,80},{64,96},{80,112},{96,128},{112,144}... | collective-permute-start | bytes 786440 | tf_op jit(solution)/shard_map/ppermute | solution.py:24
  37.4 7.3 %collective-permute-done.7 = f32[4,128,128]{2,1,0:T(8,128)S(1)} collective-permute-done((f32[4,128,128]{2,1,0:T(8,128)S(1)}, f32[4,128,128]{2,1,0:T(8,128)S(1)}, u32[]{:S(2)}, u32[]{:S(2)}) %collective-permute-start.7) | collective-permute-done | bytes 262176 | tf_op jit(solution)/shard_map/ppermute | solution.py:24
  44.7 0.1 multiply_add_fusion.2
  44.8 1.3 collective-permute-start.8
  46.2 0.7 convolution_bitcast_fusion.1
  46.9 2.3 %collective-permute-start.2 = (f32[4]{0:T(128)S(1)}, f32[4]{0:T(128)S(1)}, u32[]{:S(2)}, u32[]{:S(2)}) collective-permute-start(f32[4]{0:T(128)S(1)} %get-tuple-element.25), channel_id=1, source_target_pairs={{0,32},{16,48},{32,64},{48,80},{64,96},{80,112},{96,128},{112,144}... | collective-permute-start | bytes 56 | tf_op jit(solution)/shard_map/ppermute | solution.py:24
  49.2 4.7 %collective-permute-done.2 = f32[4]{0:T(128)S(1)} collective-permute-done((f32[4]{0:T(128)S(1)}, f32[4]{0:T(128)S(1)}, u32[]{:S(2)}, u32[]{:S(2)}) %collective-permute-start.2) | collective-permute-done | bytes 48 | tf_op jit(solution)/shard_map/ppermute | solution.py:24
  53.9 3.7 %collective-permute-done.8 = f32[4,128,128]{2,1,0:T(8,128)S(1)} collective-permute-done((f32[4,128,128]{2,1,0:T(8,128)S(1)}, f32[4,128,128]{2,1,0:T(8,128)S(1)}, u32[]{:S(2)}, u32[]{:S(2)}) %collective-permute-start.8) | collective-permute-done | bytes 262176 | tf_op jit(solution)/shard_map/ppermute | solution.py:24
  57.6 0.1 multiply_add_fusion.1
  57.7 1.3 collective-permute-start.9
  59.0 1.3 collective-permute-start.3
  60.3 7.7 %collective-permute-done.3 = f32[4]{0:T(128)S(1)} collective-permute-done((f32[4]{0:T(128)S(1)}, f32[4]{0:T(128)S(1)}, u32[]{:S(2)}, u32[]{:S(2)}) %collective-permute-start.3) | collective-permute-done | bytes 48 | tf_op jit(solution)/shard_map/ppermute | solution.py:24
  68.0 4.7 %collective-permute-done.9 = f32[4,128,128]{2,1,0:T(8,128)S(1)} collective-permute-done((f32[4,128,128]{2,1,0:T(8,128)S(1)}, f32[4,128,128]{2,1,0:T(8,128)S(1)}, u32[]{:S(2)}, u32[]{:S(2)}) %collective-permute-start.9) | collective-permute-done | bytes 262176 | tf_op jit(solution)/shard_map/ppermute | solution.py:24
  72.8 0.1 multiply_add_fusion
  72.9 1.3 collective-permute-start.10
  74.2 0.6 fusion.1
  74.7 1.3 collective-permute-start.4
  76.0 5.5 %collective-permute-done.4 = f32[4]{0:T(128)S(1)} collective-permute-done((f32[4]{0:T(128)S(1)}, f32[4]{0:T(128)S(1)}, u32[]{:S(2)}, u32[]{:S(2)}) %collective-permute-start.4) | collective-permute-done | bytes 48 | tf_op jit(solution)/shard_map/ppermute | solution.py:24
  81.6 1.1 collective-permute-done.10
  82.6 0.8 multiply_reduce_fusion
  83.4 0.2 copy.38
  83.7 39.7 %psum.7 = f32[256]{0:T(256)S(1)} all-reduce(f32[256]{0:T(256)S(1)} %get-tuple-element.40), channel_id=1, replica_groups=mesh['ctx'=32,'head'=16] {'head'}, use_global_device_ids=true, to_apply=%region_3.4 | all-reduce | flops 256 | bytes 2048 | tf_op jit(solution)/shard_map/psum | solution.py:154
  123.4 0.8 multiply_convert_fusion
  124.2 74.4 %shard_map.95 = bf16[256,512]{1,0:T(8,128)(2,1)} custom-call(s32[1]{0:T(128)} %bitcast.7.index_ref, bf16[256,512]{1,0:T(8,128)(2,1)} %q_ref.1, bf16[8192,256]{1,0:T(8,128)(2,1)} %all-gather.2.cloned.1.call-done.kv_ref), custom_call_target="tpu_custom_call" | custom-call | tf_op jit(solution)/shard_map/pallas_call | solution.py:104
  (16 shorter events, 0.1 us)
Async XLA Ops:
  7.2 39.0 %copy-start = (bf16[256,512]{1,0:T(8,128)(2,1)S(1)}, bf16[256,512]{1,0:T(8,128)(2,1)}, u32[]{:S(2)}) copy-start(bf16[256,512]{1,0:T(8,128)(2,1)} %param.8) | copy-start | bytes 786436
  7.2 67.0 %copy-start.1 = (bf16[256,512]{1,0:T(8,128)(2,1)S(1)}, bf16[256,512]{1,0:T(8,128)(2,1)}, u32[]{:S(2)}) copy-start(bf16[256,512]{1,0:T(8,128)(2,1)} %param.10) | copy-start | bytes 786436
  7.2 117.0 %all-gather.2.cloned.1.call-start = ((), (), s32[]{:S(2)}) async-start(), calls=%async_computation | async-start | bytes 4325376 | tf_op jit(solution)/shard_map/all_gather | solution.py:130
  13.7 7.7 %collective-permute-start.5 = (f32[4,128,128]{2,1,0:T(8,128)S(1)}, f32[4,128,128]{2,1,0:T(8,128)S(1)}, u32[]{:S(2)}, u32[]{:S(2)}) collective-permute-start(f32[4,128,128]{2,1,0:T(8,128)S(1)} %convolution_add_fusion), channel_id=1, source_target_pairs={{0,16},{16,32},{32,48},{48,64},{64,80},{80,96},{96,112},{112,128},... | collective-permute-start | bytes 786440 | tf_op jit(solution)/shard_map/ppermute | solution.py:24
  21.4 12.7 %collective-permute-start.6 = (f32[4,128,128]{2,1,0:T(8,128)S(1)}, f32[4,128,128]{2,1,0:T(8,128)S(1)}, u32[]{:S(2)}, u32[]{:S(2)}) collective-permute-start(f32[4,128,128]{2,1,0:T(8,128)S(1)} %collective-permute-done.5), channel_id=1, source_target_pairs={{0,16},{16,32},{32,48},{48,64},{64,80},{80,96},{96,112},{112,128},... | collective-permute-start | bytes 786440 | tf_op jit(solution)/shard_map/ppermute | solution.py:24
  23.4 5.9 %collective-permute-start = (f32[4]{0:T(128)S(1)}, f32[4]{0:T(128)S(1)}, u32[]{:S(2)}, u32[]{:S(2)}) collective-permute-start(f32[4]{0:T(128)S(1)} %slice_reduce_fusion), channel_id=1, source_target_pairs={{0,16},{16,32},{32,48},{48,64},{64,80},{80,96},{96,112},{112,128},... | collective-permute-start | bytes 56 | tf_op jit(solution)/shard_map/ppermute | solution.py:24
  29.2 4.9 %collective-permute-start.1 = (f32[4]{0:T(128)S(1)}, f32[4]{0:T(128)S(1)}, u32[]{:S(2)}, u32[]{:S(2)}) collective-permute-start(f32[4]{0:T(128)S(1)} %collective-permute-done), channel_id=1, source_target_pairs={{0,16},{16,32},{32,48},{48,64},{64,80},{80,96},{96,112},{112,128},... | collective-permute-start | bytes 56 | tf_op jit(solution)/shard_map/ppermute | solution.py:24
  34.2 10.5 %collective-permute-start.7 = (f32[4,128,128]{2,1,0:T(8,128)S(1)}, f32[4,128,128]{2,1,0:T(8,128)S(1)}, u32[]{:S(2)}, u32[]{:S(2)}) collective-permute-start(f32[4,128,128]{2,1,0:T(8,128)S(1)} %multiply_add_fusion.3), channel_id=1, source_target_pairs={{0,32},{16,48},{32,64},{48,80},{64,96},{80,112},{96,128},{112,144}... | collective-permute-start | bytes 786440 | tf_op jit(solution)/shard_map/ppermute | solution.py:24
  44.7 78.7 %copy-start.2 = (f32[512]{0:T(512)S(1)}, f32[512]{0:T(512)}, u32[]{:S(2)}) copy-start(f32[512]{0:T(512)} %param.12) | copy-start | bytes 6148
  44.8 12.7 %collective-permute-start.8 = (f32[4,128,128]{2,1,0:T(8,128)S(1)}, f32[4,128,128]{2,1,0:T(8,128)S(1)}, u32[]{:S(2)}, u32[]{:S(2)}) collective-permute-start(f32[4,128,128]{2,1,0:T(8,128)S(1)} %multiply_add_fusion.2), channel_id=1, source_target_pairs={{0,64},{16,80},{32,96},{48,112},{64,128},{80,144},{96,160},{112,17... | collective-permute-start | bytes 786440 | tf_op jit(solution)/shard_map/ppermute | solution.py:24
  46.9 7.0 %collective-permute-start.2 = (f32[4]{0:T(128)S(1)}, f32[4]{0:T(128)S(1)}, u32[]{:S(2)}, u32[]{:S(2)}) collective-permute-start(f32[4]{0:T(128)S(1)} %get-tuple-element.25), channel_id=1, source_target_pairs={{0,32},{16,48},{32,64},{48,80},{64,96},{80,112},{96,128},{112,144}... | collective-permute-start | bytes 56 | tf_op jit(solution)/shard_map/ppermute | solution.py:24
  57.7 15.1 %collective-permute-start.9 = (f32[4,128,128]{2,1,0:T(8,128)S(1)}, f32[4,128,128]{2,1,0:T(8,128)S(1)}, u32[]{:S(2)}, u32[]{:S(2)}) collective-permute-start(f32[4,128,128]{2,1,0:T(8,128)S(1)} %multiply_add_fusion.1), channel_id=1, source_target_pairs={{0,128},{16,144},{32,160},{48,176},{64,192},{80,208},{96,224},{112... | collective-permute-start | bytes 786440 | tf_op jit(solution)/shard_map/ppermute | solution.py:24
  59.0 9.0 %collective-permute-start.3 = (f32[4]{0:T(128)S(1)}, f32[4]{0:T(128)S(1)}, u32[]{:S(2)}, u32[]{:S(2)}) collective-permute-start(f32[4]{0:T(128)S(1)} %get-tuple-element.23), channel_id=1, source_target_pairs={{0,64},{16,80},{32,96},{48,112},{64,128},{80,144},{96,160},{112,17... | collective-permute-start | bytes 56 | tf_op jit(solution)/shard_map/ppermute | solution.py:24
  72.9 9.8 %collective-permute-start.10 = (f32[4,128,128]{2,1,0:T(8,128)S(1)}, f32[4,128,128]{2,1,0:T(8,128)S(1)}, u32[]{:S(2)}, u32[]{:S(2)}) collective-permute-start(f32[4,128,128]{2,1,0:T(8,128)S(1)} %multiply_add_fusion), channel_id=1, source_target_pairs={{0,256},{16,272},{32,288},{48,304},{64,320},{80,336},{96,352},{112... | collective-permute-start | bytes 786440 | tf_op jit(solution)/shard_map/ppermute | solution.py:24
  74.7 6.8 %collective-permute-start.4 = (f32[4]{0:T(128)S(1)}, f32[4]{0:T(128)S(1)}, u32[]{:S(2)}, u32[]{:S(2)}) collective-permute-start(f32[4]{0:T(128)S(1)} %get-tuple-element.21), channel_id=1, source_target_pairs={{0,128},{16,144},{32,160},{48,176},{64,192},{80,208},{96,224},{112... | collective-permute-start | bytes 56 | tf_op jit(solution)/shard_map/ppermute | solution.py:24
Sparse Core Ops, SparseCore 0:
  11.7 65.2 all-gather.1

commit v2 on v1

--- a/solution.py
+++ b/solution.py
@@ -48,59 +48,99 @@
 
 
 def exclusive_scan(log_total, block_state, axis):
-    log_acc, state_acc = shifted((log_total, block_state), axis, 1)
+    head_count, rows, cols = block_state.shape
+
+    def pack(log, state):
+        return jnp.concatenate(
+            [state, jnp.broadcast_to(log[:, None, None], (head_count, 8, cols))], axis=1
+        )
+
+    packed = shifted(pack(log_total, block_state), axis, 1)
     count = lax.axis_size(axis)
     step = 1
     while step < count:
-        log_in, state_in = shifted((log_acc, state_acc), axis, step)
-        state_acc = jnp.exp(log_acc)[:, None, None] * state_in + state_acc
-        log_acc = log_acc + log_in
+        incoming = shifted(packed, axis, step)
+        log_acc = packed[:, rows, 0]
+        state = jnp.exp(log_acc)[:, None, None] * incoming[:, :rows] + packed[:, :rows]
+        packed = pack(log_acc + incoming[:, rows, 0], state)
         step *= 2
-    return state_acc
-
-
-def soft_kernel(index_ref, q_ref, kv_ref, o_ref, max_ref, total_ref, acc_ref):
+    return packed[:, :rows]
+
+
+def ring_sum(value, axis):
+    count = lax.axis_size(axis)
+    if count & (count - 1):
+        return lax.psum(value, axis)
+    total = value
+    step = 1
+    while step < count:
+        total = total + lax.ppermute(
+            total, axis, [(source, (source + step) % count) for source in range(count)]
+        )
+        step *= 2
+    return total
+
+
+def soft_kernel(index_ref, q_ref, kv_ref, vt_ref, o_ref, max_ref, total_ref, acc_ref):
     my_index = index_ref[0]
-    row_count = q_ref.shape[0]
-    head_count = q_ref.shape[1] // DH
+    row_count = o_ref.shape[0]
+    head_count = o_ref.shape[1] // DH
+    wide = q_ref.shape[0]
     max_ref[...] = jnp.full(max_ref.shape, NEGATIVE, jnp.float32)
     total_ref[...] = jnp.zeros(total_ref.shape, jnp.float32)
     acc_ref[...] = jnp.zeros(acc_ref.shape, jnp.float32)
-    query_pos = my_index * row_count + lax.broadcasted_iota(jnp.int32, (row_count, KEY_BLOCK), 0)
+    full_blocks = (my_index * row_count) // KEY_BLOCK
     block_count = (my_index * row_count + row_count - 1) // KEY_BLOCK + 1
 
-    def body(block, carry):
+    def update(block, masked):
         start = pl.multiple_of(block * KEY_BLOCK, KEY_BLOCK)
         keys = kv_ref[pl.ds(start, KEY_BLOCK), 0:DH]
-        values = kv_ref[pl.ds(start, KEY_BLOCK), DH : 2 * DH]
-        key_pos = start + lax.broadcasted_iota(jnp.int32, (row_count, KEY_BLOCK), 1)
-        allowed = key_pos <= query_pos
-        for head in range(head_count):
-            queries = q_ref[:, head * DH : (head + 1) * DH]
-            scores = lax.dot_general(
-                queries, keys, (((1,), (1,)), ((), ())), preferred_element_type=jnp.float32
-            ) * DH ** (-0.5)
+        values_t = vt_ref[:, pl.ds(start, KEY_BLOCK)]
+        scores = lax.dot_general(
+            keys, q_ref[...], (((1,), (1,)), ((), ())), preferred_element_type=jnp.float32
+        ) * DH ** (-0.5)
+        if masked:
+            key_pos = start + lax.broadcasted_iota(jnp.int32, (KEY_BLOCK, wide), 0)
+            query_pos = my_index * row_count + lax.rem(
+                lax.broadcasted_iota(jnp.int32, (KEY_BLOCK, wide), 1), row_count
+            )
+            allowed = key_pos <= query_pos
             scores = jnp.where(allowed, scores, NEGATIVE)
-            row_max = max_ref[head]
-            new_max = jnp.maximum(row_max, jnp.max(scores, axis=1, keepdims=True))
-            probabilities = jnp.where(allowed, jnp.exp(scores - new_max), 0.0)
-            rescale = jnp.exp(row_max - new_max)
-            total_ref[head] = total_ref[head] * rescale + jnp.sum(probabilities, axis=1, keepdims=True)
-            product = jnp.dot(
-                probabilities.astype(jnp.bfloat16), values, preferred_element_type=jnp.float32
-            )
-            acc_ref[head] = acc_ref[head] * rescale + product
-            max_ref[head] = new_max
+        row_max = max_ref[...]
+        new_max = jnp.maximum(row_max, jnp.max(scores, axis=0, keepdims=True))
+        probabilities = jnp.exp(scores - new_max)
+        if masked:
+            probabilities = jnp.where(allowed, probabilities, 0.0)
+        rescale = jnp.exp(row_max - new_max)
+        total_ref[...] = total_ref[...] * rescale + jnp.sum(probabilities, axis=0, keepdims=True)
+        product = jnp.dot(
+            values_t, probabilities.astype(jnp.bfloat16), preferred_element_type=jnp.float32
+        )
+        acc_ref[...] = acc_ref[...] * rescale + product
+        max_ref[...] = new_max
+
+    def plain(block, carry):
+        update(block, False)
         return carry
 
-    lax.fori_loop(0, block_count, body, 0)
+    def diagonal(block, carry):
+        update(block, True)
+        return carry
+
+    lax.fori_loop(0, full_blocks, plain, 0)
+    lax.fori_loop(full_blocks, block_count, diagonal, 0)
     for head in range(head_count):
-        o_ref[:, head * DH : (head + 1) * DH] = (acc_ref[head] / total_ref[head]).astype(o_ref.dtype)
+        cols = slice(head * row_count, (head + 1) * row_count)
+        ratio = acc_ref[:, cols] / total_ref[:, cols]
+        o_ref[:, head * DH : (head + 1) * DH] = ratio.T.astype(o_ref.dtype)
 
 
 def soft_attention(my_index, queries, keys_values):
     row_count, width = queries.shape
     head_count = width // DH
+    wide = head_count * row_count
+    stacked = queries.reshape(row_count, head_count, DH).transpose(1, 0, 2).reshape(wide, DH)
+    values_t = keys_values[:, DH : 2 * DH].T
     return pl.pallas_call(
         soft_kernel,
         out_shape=jax.ShapeDtypeStruct((row_count, width), jnp.bfloat16),
@@ -108,14 +148,15 @@
             pl.BlockSpec(memory_space=pltpu.SMEM),
             pl.BlockSpec(memory_space=pltpu.VMEM),
             pl.BlockSpec(memory_space=pltpu.VMEM),
+            pl.BlockSpec(memory_space=pltpu.VMEM),
         ],
         out_specs=pl.BlockSpec(memory_space=pltpu.VMEM),
         scratch_shapes=[
-            pltpu.VMEM((head_count, row_count, 1), jnp.float32),
-            pltpu.VMEM((head_count, row_count, 1), jnp.float32),
-            pltpu.VMEM((head_count, row_count, DH), jnp.float32),
+            pltpu.VMEM((1, wide), jnp.float32),
+            pltpu.VMEM((1, wide), jnp.float32),
+            pltpu.VMEM((DH, wide), jnp.float32),
         ],
-    )(my_index.reshape(1), queries, keys_values)
+    )(my_index.reshape(1), stacked, keys_values, values_t)
 
 
 def local(q_linear, k_linear, v_linear, log_decay, norm_gain, q_soft, k_soft, v_soft):
@@ -151,7 +192,7 @@
     entering = exclusive_scan(log_total, block_state, "ctx")
     carried = jnp.einsum("thd,hde->the", lifted, entering, precision=lax.Precision.HIGHEST)
     mixed = (local_part + carried).reshape(row_count, width)
-    power = lax.psum(jnp.sum(mixed * mixed, axis=1), "head") / (QUERY_HEADS * DH)
+    power = ring_sum(jnp.sum(mixed * mixed, axis=1), "head") / (QUERY_HEADS * DH)
     linear_out = (mixed * lax.rsqrt(power + EPSILON)[:, None] * norm_gain[None, :]).astype(
         jnp.bfloat16
     )

time: 206 us -> 170 us (0.83)
  the two profiles are of different devices: /device:TPU:22 before, /device:TPU:30 now
where the time goes in v2:
time: 170 us; the launch traced here: 169 us
  waiting for transfers between devices  74.8 us (44%)
  starting transfers between devices  30.9 us (18%)
  Pallas kernels  27.7 us (16%)
  local copies, waits for them, and re-layouts  14.5 us (9%)
  between operations  14.3 us (8%)
  other arithmetic  3.7 us (2%)
  matrix products  3.29 us (2%)
    ppermute x6, waiting for transfers between devices, shifted(): lax.ppermute(value, axis, [(source, source + steps) for source in range(f...  52.6 us
    pallas_call x1, Pallas kernels, soft_attention(): pl.pallas_call(soft_kernel, out_shape=jax.ShapeDtypeStruct((row_count, wi...  27.7 us
    ppermute x4, waiting for transfers between devices, ring_sum(): lax.ppermute(total, axis, [(source, (source + step) % count) for source i...  22.2 us
    ppermute x4, starting transfers between devices, ring_sum(): lax.ppermute(total, axis, [(source, (source + step) % count) for source i...  21.8 us
    ppermute x6, starting transfers between devices, shifted(): lax.ppermute(value, axis, [(source, source + steps) for source in range(f...  9.13 us
    all_gather x1, local copies, waits for them, and re-layouts, local(): lax.all_gather(jnp.concatenate([k_local, v_local], axis=1), 'ctx', axis=0...  6.38 us
  transfers between devices with their start and end apart: 11, of which 10 were waited for; matrix products, arithmetic and copies ran while one was open for 6% of the time, Pallas kernels for 0%

profile of v2, /device:TPU:30, one launch (start us, length us, event | category | flops | bytes accessed | tf_op | source)
XLA Modules:
  0.0 169.2 jit_solution(2324704847011848407)
XLA Ops:
  7.2 0.9 constant_dynamic-slice_fusion
  8.1 0.1 copy.69
  8.3 0.1 copy.70
  8.4 0.7 pad_maximum_fusion.5
  9.1 0.7 reshape.94
  9.8 1.2 reduce-window.6
  11.1 0.1 copy.56
  11.2 0.1 copy.57
  11.4 1.1 copy.71
  12.5 0.2 slice_reduce_fusion
  12.8 1.2 convolution_add_fusion
  14.0 1.9 %collective-permute-start = (f32[4,136,128]{2,1,0:T(8,128)S(1)}, f32[4,136,128]{2,1,0:T(8,128)S(1)}, u32[]{:S(2)}, u32[]{:S(2)}) collective-permute-start(f32[4,136,128]{2,1,0:T(8,128)S(1)} %pad_maximum_fusion), channel_id=1, source_target_pairs={{0,16},{16,32},{32,48},{48,64},{64,80},{80,96},{96,112},{112,128},... | collective-permute-start | bytes 835592 | tf_op jit(solution)/shard_map/ppermute | solution.py:24
  16.0 5.9 %collective-permute-done = f32[4,136,128]{2,1,0:T(8,128)S(1)} collective-permute-done((f32[4,136,128]{2,1,0:T(8,128)S(1)}, f32[4,136,128]{2,1,0:T(8,128)S(1)}, u32[]{:S(2)}, u32[]{:S(2)}) %collective-permute-start) | collective-permute-done | bytes 278560 | tf_op jit(solution)/shard_map/ppermute | solution.py:24
  21.9 1.9 %collective-permute-start.1 = (f32[4,136,128]{2,1,0:T(8,128)S(1)}, f32[4,136,128]{2,1,0:T(8,128)S(1)}, u32[]{:S(2)}, u32[]{:S(2)}) collective-permute-start(f32[4,136,128]{2,1,0:T(8,128)S(1)} %collective-permute-done), channel_id=1, source_target_pairs={{0,16},{16,32},{32,48},{48,64},{64,80},{80,96},{96,112},{112,128},... | collective-permute-start | bytes 835592 | tf_op jit(solution)/shard_map/ppermute | solution.py:24
  23.8 5.9 %collective-permute-done.1 = f32[4,136,128]{2,1,0:T(8,128)S(1)} collective-permute-done((f32[4,136,128]{2,1,0:T(8,128)S(1)}, f32[4,136,128]{2,1,0:T(8,128)S(1)}, u32[]{:S(2)}, u32[]{:S(2)}) %collective-permute-start.1) | collective-permute-done | bytes 278560 | tf_op jit(solution)/shard_map/ppermute | solution.py:24
  29.8 0.1 fusion.37
  29.9 0.1 slice_add_fusion
  30.1 1.3 collective-permute-start.2
  31.4 8.4 %collective-permute-done.2 = f32[4,136,128]{2,1,0:T(8,128)S(1)} collective-permute-done((f32[4,136,128]{2,1,0:T(8,128)S(1)}, f32[4,136,128]{2,1,0:T(8,128)S(1)}, u32[]{:S(2)}, u32[]{:S(2)}) %collective-permute-start.2) | collective-permute-done | bytes 278560 | tf_op jit(solution)/shard_map/ppermute | solution.py:24
  39.8 0.1 slice_reduce_fusion.3
  39.9 0.1 fusion.20
  40.1 1.4 collective-permute-start.3
  41.6 8.6 %collective-permute-done.3 = f32[4,136,128]{2,1,0:T(8,128)S(1)} collective-permute-done((f32[4,136,128]{2,1,0:T(8,128)S(1)}, f32[4,136,128]{2,1,0:T(8,128)S(1)}, u32[]{:S(2)}, u32[]{:S(2)}) %collective-permute-start.3) | collective-permute-done | bytes 278560 | tf_op jit(solution)/shard_map/ppermute | solution.py:24
  50.2 0.1 slice_reduce_fusion.2
  50.3 0.1 fusion.19
  50.5 1.3 collective-permute-start.4
  51.9 0.7 convolution_bitcast_fusion.1
  52.6 11.8 %collective-permute-done.4 = f32[4,136,128]{2,1,0:T(8,128)S(1)} collective-permute-done((f32[4,136,128]{2,1,0:T(8,128)S(1)}, f32[4,136,128]{2,1,0:T(8,128)S(1)}, u32[]{:S(2)}, u32[]{:S(2)}) %collective-permute-start.4) | collective-permute-done | bytes 278560 | tf_op jit(solution)/shard_map/ppermute | solution.py:24
  64.4 0.1 exponential_reduce_fusion
  64.5 0.1 fusion.18
  64.7 1.3 collective-permute-start.5
  66.0 0.6 fusion.1
  66.6 11.9 %collective-permute-done.5 = f32[4,136,128]{2,1,0:T(8,128)S(1)} collective-permute-done((f32[4,136,128]{2,1,0:T(8,128)S(1)}, f32[4,136,128]{2,1,0:T(8,128)S(1)}, u32[]{:S(2)}, u32[]{:S(2)}) %collective-permute-start.5) | collective-permute-done | bytes 278560 | tf_op jit(solution)/shard_map/ppermute | solution.py:24
  78.5 0.8 multiply_reduce_fusion
  79.3 6.0 %collective-permute-start.6 = (f32[256]{0:T(256)S(1)}, f32[256]{0:T(256)S(1)}, u32[]{:S(2)}, u32[]{:S(2)}) collective-permute-start(f32[256]{0:T(256)S(1)} %get-tuple-element.43), channel_id=1, source_target_pairs={{0,1},{1,2},{2,3},{3,4},{4,5},{5,6},{6,7},{7,8},{8,9},{9,10},{10,1... | collective-permute-start | bytes 3080 | tf_op jit(solution)/shard_map/ppermute | solution.py:77
  85.3 7.9 %collective-permute-done.6 = f32[256]{0:T(256)S(1)} collective-permute-done((f32[256]{0:T(256)S(1)}, f32[256]{0:T(256)S(1)}, u32[]{:S(2)}, u32[]{:S(2)}) %collective-permute-start.6) | collective-permute-done | bytes 1056 | tf_op jit(solution)/shard_map/ppermute | solution.py:77
  93.2 1.9 %collective-permute-start.7 = (f32[256]{0:T(256)S(1)}, f32[256]{0:T(256)S(1)}, u32[]{:S(2)}, u32[]{:S(2)}) collective-permute-start(f32[256]{0:T(256)S(1)} %add.101), channel_id=1, source_target_pairs={{0,2},{1,3},{2,4},{3,5},{4,6},{5,7},{6,8},{7,9},{8,10},{9,11},{10,... | collective-permute-start | bytes 3080 | tf_op jit(solution)/shard_map/ppermute | solution.py:77
  95.1 5.6 %collective-permute-done.7 = f32[256]{0:T(256)S(1)} collective-permute-done((f32[256]{0:T(256)S(1)}, f32[256]{0:T(256)S(1)}, u32[]{:S(2)}, u32[]{:S(2)}) %collective-permute-start.7) | collective-permute-done | bytes 1056 | tf_op jit(solution)/shard_map/ppermute | solution.py:77
  100.8 2.9 %collective-permute-start.8 = (f32[256]{0:T(256)S(1)}, f32[256]{0:T(256)S(1)}, u32[]{:S(2)}, u32[]{:S(2)}) collective-permute-start(f32[256]{0:T(256)S(1)} %add.102), channel_id=1, source_target_pairs={{0,4},{1,5},{2,6},{3,7},{4,8},{5,9},{6,10},{7,11},{8,12},{9,13},{1... | collective-permute-start | bytes 3080 | tf_op jit(solution)/shard_map/ppermute | solution.py:77
  103.6 6.5 %collective-permute-done.8 = f32[256]{0:T(256)S(1)} collective-permute-done((f32[256]{0:T(256)S(1)}, f32[256]{0:T(256)S(1)}, u32[]{:S(2)}, u32[]{:S(2)}) %collective-permute-start.8) | collective-permute-done | bytes 1056 | tf_op jit(solution)/shard_map/ppermute | solution.py:77
  110.1 11.0 %collective-permute-start.9 = (f32[256]{0:T(256)S(1)}, f32[256]{0:T(256)S(1)}, u32[]{:S(2)}, u32[]{:S(2)}) collective-permute-start(f32[256]{0:T(256)S(1)} %add.103), channel_id=1, source_target_pairs={{0,8},{1,9},{2,10},{3,11},{4,12},{5,13},{6,14},{7,15},{8,0},{9,1},... | collective-permute-start | bytes 3080 | tf_op jit(solution)/shard_map/ppermute | solution.py:77
  121.2 0.8 copy_bitcast_fusion
  122.0 0.2 copy.63
  122.2 2.1 %collective-permute-done.9 = f32[256]{0:T(256)S(1)} collective-permute-done((f32[256]{0:T(256)S(1)}, f32[256]{0:T(256)S(1)}, u32[]{:S(2)}, u32[]{:S(2)}) %collective-permute-start.9) | collective-permute-done | bytes 1056 | tf_op jit(solution)/shard_map/ppermute | solution.py:77
  124.3 0.8 multiply_convert_fusion
  125.1 6.4 %copy.67.kv_ref = bf16[8192,256]{1,0:T(8,128)(2,1)} copy(bf16[8192,256]{0,1:T(8,128)(2,1)} %all-gather.2.cloned.1.call-done) | data formatting | bytes 8388608 | tf_op jit(solution)/shard_map/all_gather | solution.py:171
  131.5 3.2 %slice_bitcast_fusion.vt_ref = bf16[128,8192]{1,0:T(8,128)(2,1)} fusion(bf16[8192,256]{0,1:T(8,128)(2,1)} %all-gather.2.cloned.1.call-done), kind=kLoop, calls=%fused_computation | loop fusion | bytes 4194304 | tf_op jit(solution)/shard_map/transpose | solution.py:143
  134.7 27.7 %shard_map.95 = bf16[256,512]{1,0:T(8,128)(2,1)} custom-call(s32[1]{0:T(128)} %bitcast.7.index_ref, bf16[1024,128]{1,0:T(8,128)(2,1)} %bitcast.80, bf16[8192,256]{1,0:T(8,128)(2,1)} %copy.67.kv_ref, bf16[128,8192]{1,0:T(8,128)(2,1)} %slice_bitcast_fusion.vt_ref), custom_call_target="tpu_custom_call" | custom-call | tf_op jit(solution)/shard_map/pallas_call | solution.py:144
  (36 shorter events, 0.9 us)
Async XLA Ops:
  7.2 44.7 %copy-start = (bf16[256,512]{1,0:T(8,128)(2,1)S(1)}, bf16[256,512]{1,0:T(8,128)(2,1)}, u32[]{:S(2)}) copy-start(bf16[256,512]{1,0:T(8,128)(2,1)} %param.8) | copy-start | bytes 786436
  7.2 117.9 %all-gather.2.cloned.1.call-start = ((), (), s32[]{:S(2)}) async-start(), calls=%async_computation | async-start | bytes 4325376 | tf_op jit(solution)/shard_map/all_gather | solution.py:171
  9.0 57.0 %copy-start.2 = (bf16[256,512]{1,0:T(8,128)(2,1)S(1)}, bf16[256,512]{1,0:T(8,128)(2,1)}, u32[]{:S(2)}) copy-start(bf16[256,512]{1,0:T(8,128)(2,1)} %param.10) | copy-start | bytes 786436
  14.0 7.9 %collective-permute-start = (f32[4,136,128]{2,1,0:T(8,128)S(1)}, f32[4,136,128]{2,1,0:T(8,128)S(1)}, u32[]{:S(2)}, u32[]{:S(2)}) collective-permute-start(f32[4,136,128]{2,1,0:T(8,128)S(1)} %pad_maximum_fusion), channel_id=1, source_target_pairs={{0,16},{16,32},{32,48},{48,64},{64,80},{80,96},{96,112},{112,128},... | collective-permute-start | bytes 835592 | tf_op jit(solution)/shard_map/ppermute | solution.py:24
  21.9 7.9 %collective-permute-start.1 = (f32[4,136,128]{2,1,0:T(8,128)S(1)}, f32[4,136,128]{2,1,0:T(8,128)S(1)}, u32[]{:S(2)}, u32[]{:S(2)}) collective-permute-start(f32[4,136,128]{2,1,0:T(8,128)S(1)} %collective-permute-done), channel_id=1, source_target_pairs={{0,16},{16,32},{32,48},{48,64},{64,80},{80,96},{96,112},{112,128},... | collective-permute-start | bytes 835592 | tf_op jit(solution)/shard_map/ppermute | solution.py:24
  30.1 9.7 %collective-permute-start.2 = (f32[4,136,128]{2,1,0:T(8,128)S(1)}, f32[4,136,128]{2,1,0:T(8,128)S(1)}, u32[]{:S(2)}, u32[]{:S(2)}) collective-permute-start(f32[4,136,128]{2,1,0:T(8,128)S(1)} %pad_maximum_fusion.1), channel_id=1, source_target_pairs={{0,32},{16,48},{32,64},{48,80},{64,96},{80,112},{96,128},{112,144}... | collective-permute-start | bytes 835592 | tf_op jit(solution)/shard_map/ppermute | solution.py:24
  40.1 81.1 %copy-start.1 = (bf16[256,512]{1,0:T(8,128)(2,1)S(1)}, bf16[256,512]{1,0:T(8,128)(2,1)}, u32[]{:S(2)}) copy-start(bf16[256,512]{1,0:T(8,128)(2,1)} %param.13) | copy-start | bytes 786436
  40.1 10.1 %collective-permute-start.3 = (f32[4,136,128]{2,1,0:T(8,128)S(1)}, f32[4,136,128]{2,1,0:T(8,128)S(1)}, u32[]{:S(2)}, u32[]{:S(2)}) collective-permute-start(f32[4,136,128]{2,1,0:T(8,128)S(1)} %pad_maximum_fusion.2), channel_id=1, source_target_pairs={{0,64},{16,80},{32,96},{48,112},{64,128},{80,144},{96,160},{112,17... | collective-permute-start | bytes 835592 | tf_op jit(solution)/shard_map/ppermute | solution.py:24
  50.5 73.8 %copy-start.3 = (f32[512]{0:T(512)S(1)}, f32[512]{0:T(512)}, u32[]{:S(2)}) copy-start(f32[512]{0:T(512)} %param.12) | copy-start | bytes 6148
  50.5 13.8 %collective-permute-start.4 = (f32[4,136,128]{2,1,0:T(8,128)S(1)}, f32[4,136,128]{2,1,0:T(8,128)S(1)}, u32[]{:S(2)}, u32[]{:S(2)}) collective-permute-start(f32[4,136,128]{2,1,0:T(8,128)S(1)} %pad_maximum_fusion.3), channel_id=1, source_target_pairs={{0,128},{16,144},{32,160},{48,176},{64,192},{80,208},{96,224},{112... | collective-permute-start | bytes 835592 | tf_op jit(solution)/shard_map/ppermute | solution.py:24
  64.7 13.8 %collective-permute-start.5 = (f32[4,136,128]{2,1,0:T(8,128)S(1)}, f32[4,136,128]{2,1,0:T(8,128)S(1)}, u32[]{:S(2)}, u32[]{:S(2)}) collective-permute-start(f32[4,136,128]{2,1,0:T(8,128)S(1)} %pad_maximum_fusion.4), channel_id=1, source_target_pairs={{0,256},{16,272},{32,288},{48,304},{64,320},{80,336},{96,352},{112... | collective-permute-start | bytes 835592 | tf_op jit(solution)/shard_map/ppermute | solution.py:24
  79.3 13.8 %collective-permute-start.6 = (f32[256]{0:T(256)S(1)}, f32[256]{0:T(256)S(1)}, u32[]{:S(2)}, u32[]{:S(2)}) collective-permute-start(f32[256]{0:T(256)S(1)} %get-tuple-element.43), channel_id=1, source_target_pairs={{0,1},{1,2},{2,3},{3,4},{4,5},{5,6},{6,7},{7,8},{8,9},{9,10},{10,1... | collective-permute-start | bytes 3080 | tf_op jit(solution)/shard_map/ppermute | solution.py:77
  93.2 7.6 %collective-permute-start.7 = (f32[256]{0:T(256)S(1)}, f32[256]{0:T(256)S(1)}, u32[]{:S(2)}, u32[]{:S(2)}) collective-permute-start(f32[256]{0:T(256)S(1)} %add.101), channel_id=1, source_target_pairs={{0,2},{1,3},{2,4},{3,5},{4,6},{5,7},{6,8},{7,9},{8,10},{9,11},{10,... | collective-permute-start | bytes 3080 | tf_op jit(solution)/shard_map/ppermute | solution.py:77
  100.8 9.4 %collective-permute-start.8 = (f32[256]{0:T(256)S(1)}, f32[256]{0:T(256)S(1)}, u32[]{:S(2)}, u32[]{:S(2)}) collective-permute-start(f32[256]{0:T(256)S(1)} %add.102), channel_id=1, source_target_pairs={{0,4},{1,5},{2,6},{3,7},{4,8},{5,9},{6,10},{7,11},{8,12},{9,13},{1... | collective-permute-start | bytes 3080 | tf_op jit(solution)/shard_map/ppermute | solution.py:77
  110.1 14.2 %collective-permute-start.9 = (f32[256]{0:T(256)S(1)}, f32[256]{0:T(256)S(1)}, u32[]{:S(2)}, u32[]{:S(2)}) collective-permute-start(f32[256]{0:T(256)S(1)} %add.103), channel_id=1, source_target_pairs={{0,8},{1,9},{2,10},{3,11},{4,12},{5,13},{6,14},{7,15},{8,0},{9,1},... | collective-permute-start | bytes 3080 | tf_op jit(solution)/shard_map/ppermute | solution.py:77
Sparse Core Ops, SparseCore 0:
  11.6 70.6 all-gather.1

commit v3 on v2

--- a/solution.py
+++ b/solution.py
@@ -1,11 +1,10 @@
-import functools
-
 import jax
 import jax.numpy as jnp
 from jax import lax
 from jax.experimental import pallas as pl
 from jax.experimental.pallas import tpu as pltpu
 from jax.sharding import PartitionSpec as P
+
 
 QUERY_HEADS = 64
 DH = 128
@@ -55,33 +54,37 @@
             [state, jnp.broadcast_to(log[:, None, None], (head_count, 8, cols))], axis=1
         )
 
-    packed = shifted(pack(log_total, block_state), axis, 1)
     count = lax.axis_size(axis)
+    window_log, window_state = None, None
     step = 1
     while step < count:
-        incoming = shifted(packed, axis, step)
-        log_acc = packed[:, rows, 0]
-        state = jnp.exp(log_acc)[:, None, None] * incoming[:, :rows] + packed[:, :rows]
-        packed = pack(log_acc + incoming[:, rows, 0], state)
+        if window_log is None:
+            sent_log, sent_state = log_total, block_state
+        else:
+            sent_state = jnp.exp(log_total)[:, None, None] * window_state + block_state
+            sent_log = window_log + log_total
+        incoming = shifted(pack(sent_log, sent_state), axis, step)
+        incoming_log, incoming_state = incoming[:, rows, 0], incoming[:, :rows]
+        if window_log is None:
+            window_log, window_state = incoming_log, incoming_state
+        else:
+            window_state = jnp.exp(window_log)[:, None, None] * incoming_state + window_state
+            window_log = window_log + incoming_log
         step *= 2
-    return packed[:, :rows]
-
-
-def ring_sum(value, axis):
+    return window_state
+
+
+def all_sum(value, axis):
     count = lax.axis_size(axis)
-    if count & (count - 1):
-        return lax.psum(value, axis)
     total = value
-    step = 1
-    while step < count:
+    for distance in range(1, count):
         total = total + lax.ppermute(
-            total, axis, [(source, (source + step) % count) for source in range(count)]
+            value, axis, [(source, (source + distance) % count) for source in range(count)]
         )
-        step *= 2
     return total
 
 
-def soft_kernel(index_ref, q_ref, kv_ref, vt_ref, o_ref, max_ref, total_ref, acc_ref):
+def soft_kernel(index_ref, q_ref, kvt_ref, o_ref, max_ref, total_ref, acc_ref):
     my_index = index_ref[0]
     row_count = o_ref.shape[0]
     head_count = o_ref.shape[1] // DH
@@ -94,10 +97,10 @@
 
     def update(block, masked):
         start = pl.multiple_of(block * KEY_BLOCK, KEY_BLOCK)
-        keys = kv_ref[pl.ds(start, KEY_BLOCK), 0:DH]
-        values_t = vt_ref[:, pl.ds(start, KEY_BLOCK)]
+        keys_t = kvt_ref[0:DH, pl.ds(start, KEY_BLOCK)]
+        values_t = kvt_ref[DH : 2 * DH, pl.ds(start, KEY_BLOCK)]
         scores = lax.dot_general(
-            keys, q_ref[...], (((1,), (1,)), ((), ())), preferred_element_type=jnp.float32
+            keys_t, q_ref[...], (((0,), (1,)), ((), ())), preferred_element_type=jnp.float32
         ) * DH ** (-0.5)
         if masked:
             key_pos = start + lax.broadcasted_iota(jnp.int32, (KEY_BLOCK, wide), 0)
@@ -140,13 +143,12 @@
     head_count = width // DH
     wide = head_count * row_count
     stacked = queries.reshape(row_count, head_count, DH).transpose(1, 0, 2).reshape(wide, DH)
-    values_t = keys_values[:, DH : 2 * DH].T
+    keys_values_t = keys_values.T
     return pl.pallas_call(
         soft_kernel,
         out_shape=jax.ShapeDtypeStruct((row_count, width), jnp.bfloat16),
         in_specs=[
             pl.BlockSpec(memory_space=pltpu.SMEM),
-            pl.BlockSpec(memory_space=pltpu.VMEM),
             pl.BlockSpec(memory_space=pltpu.VMEM),
             pl.BlockSpec(memory_space=pltpu.VMEM),
         ],
@@ -156,10 +158,10 @@
             pltpu.VMEM((1, wide), jnp.float32),
             pltpu.VMEM((DH, wide), jnp.float32),
         ],
-    )(my_index.reshape(1), stacked, keys_values, values_t)
-
-
-def local(q_linear, k_linear, v_linear, log_decay, norm_gain, q_soft, k_soft, v_soft):
+    )(my_index.reshape(1), stacked, keys_values_t)
+
+
+def layer(q_linear, k_linear, v_linear, log_decay, norm_gain, q_soft, k_soft, v_soft):
     row_count = q_linear.shape[0]
     head_count = log_decay.shape[1]
     width = head_count * DH
@@ -192,7 +194,7 @@
     entering = exclusive_scan(log_total, block_state, "ctx")
     carried = jnp.einsum("thd,hde->the", lifted, entering, precision=lax.Precision.HIGHEST)
     mixed = (local_part + carried).reshape(row_count, width)
-    power = ring_sum(jnp.sum(mixed * mixed, axis=1), "head") / (QUERY_HEADS * DH)
+    power = all_sum(jnp.sum(mixed * mixed, axis=1), "head") / (QUERY_HEADS * DH)
     linear_out = (mixed * lax.rsqrt(power + EPSILON)[:, None] * norm_gain[None, :]).astype(
         jnp.bfloat16
     )
@@ -207,7 +209,7 @@
 
 def solution(mesh):
     return jax.shard_map(
-        local,
+        layer,
         mesh=mesh,
         in_specs=(
             P("ctx", "head"),

time: 170 us -> 187 us (1.10)
  the two profiles are of different devices: /device:TPU:30 before, /device:TPU:6 now
where the time goes in v3:
time: 187 us; the launch traced here: 186 us
  starting transfers between devices  92.8 us (50%)
  waiting for transfers between devices  43.9 us (23%)
  Pallas kernels  23.1 us (12%)
  between operations  14.5 us (8%)
  local copies, waits for them, and re-layouts  4.66 us (2%)
  other arithmetic  3.97 us (2%)
  matrix products  3.28 us (2%)
    ppermute x15, starting transfers between devices, all_sum(): lax.ppermute(value, axis, [(source, (source + distance) % count) for sour...  84.3 us
    ppermute x5, waiting for transfers between devices, shifted(): lax.ppermute(value, axis, [(source, source + steps) for source in range(f...  40.4 us
    pallas_call x1, Pallas kernels, soft_attention(): pl.pallas_call(soft_kernel, out_shape=jax.ShapeDtypeStruct((row_count, wi...  23.1 us
    ppermute x5, starting transfers between devices, shifted(): lax.ppermute(value, axis, [(source, source + steps) for source in range(f...  8.48 us
  transfers between devices with their start and end apart: 21, of which 6 were waited for; matrix products, arithmetic and copies ran while one was open for 5% of the time, Pallas kernels for 0%

profile of v3, /device:TPU:6, one launch (start us, length us, event | category | flops | bytes accessed | tf_op | source)
XLA Modules:
  0.0 186.3 jit_solution(327393937315652073)
XLA Ops:
  7.2 0.9 constant_dynamic-slice_fusion
  8.1 0.1 copy.81
  8.4 0.7 pad_maximum_fusion.5
  9.1 0.7 reshape.90
  9.8 1.2 reduce-window.6
  11.4 1.1 copy.83
  12.5 0.2 fusion.37
  12.7 1.2 convolution_add_fusion
  14.0 2.1 %collective-permute-start = (f32[4,136,128]{2,1,0:T(8,128)S(1)}, f32[4,136,128]{2,1,0:T(8,128)S(1)}, u32[]{:S(2)}, u32[]{:S(2)}) collective-permute-start(f32[4,136,128]{2,1,0:T(8,128)S(1)} %pad_maximum_fusion), channel_id=1, source_target_pairs={{0,16},{16,32},{32,48},{48,64},{64,80},{80,96},{96,112},{112,128},... | collective-permute-start | bytes 835592 | tf_op jit(solution)/shard_map/ppermute | solution.py:23
  16.1 8.0 %collective-permute-done = f32[4,136,128]{2,1,0:T(8,128)S(1)} collective-permute-done((f32[4,136,128]{2,1,0:T(8,128)S(1)}, f32[4,136,128]{2,1,0:T(8,128)S(1)}, u32[]{:S(2)}, u32[]{:S(2)}) %collective-permute-start) | collective-permute-done | bytes 278560 | tf_op jit(solution)/shard_map/ppermute | solution.py:23
  24.1 0.1 exponential_reduce_fusion.3
  24.4 1.9 %collective-permute-start.1 = (f32[4,136,128]{2,1,0:T(8,128)S(1)}, f32[4,136,128]{2,1,0:T(8,128)S(1)}, u32[]{:S(2)}, u32[]{:S(2)}) collective-permute-start(f32[4,136,128]{2,1,0:T(8,128)S(1)} %pad_maximum_fusion.1), channel_id=1, source_target_pairs={{0,32},{16,48},{32,64},{48,80},{64,96},{80,112},{96,128},{112,144}... | collective-permute-start | bytes 835592 | tf_op jit(solution)/shard_map/ppermute | solution.py:23
  26.4 8.6 %collective-permute-done.1 = f32[4,136,128]{2,1,0:T(8,128)S(1)} collective-permute-done((f32[4,136,128]{2,1,0:T(8,128)S(1)}, f32[4,136,128]{2,1,0:T(8,128)S(1)}, u32[]{:S(2)}, u32[]{:S(2)}) %collective-permute-start.1) | collective-permute-done | bytes 278560 | tf_op jit(solution)/shard_map/ppermute | solution.py:23
  35.0 0.1 exponential_reduce_fusion.2
  35.1 0.1 multiply_add_fusion.2
  35.3 1.9 %collective-permute-start.2 = (f32[4,136,128]{2,1,0:T(8,128)S(1)}, f32[4,136,128]{2,1,0:T(8,128)S(1)}, u32[]{:S(2)}, u32[]{:S(2)}) collective-permute-start(f32[4,136,128]{2,1,0:T(8,128)S(1)} %pad_maximum_fusion.2), channel_id=1, source_target_pairs={{0,64},{16,80},{32,96},{48,112},{64,128},{80,144},{96,160},{112,17... | collective-permute-start | bytes 835592 | tf_op jit(solution)/shard_map/ppermute | solution.py:23
  37.3 9.4 %collective-permute-done.2 = f32[4,136,128]{2,1,0:T(8,128)S(1)} collective-permute-done((f32[4,136,128]{2,1,0:T(8,128)S(1)}, f32[4,136,128]{2,1,0:T(8,128)S(1)}, u32[]{:S(2)}, u32[]{:S(2)}) %collective-permute-start.2) | collective-permute-done | bytes 278560 | tf_op jit(solution)/shard_map/ppermute | solution.py:23
  46.6 0.1 add_reduce_fusion.1
  46.7 0.1 multiply_add_fusion.1
  47.0 1.3 collective-permute-start.3
  48.3 0.7 convolution_bitcast_fusion.1
  49.0 6.4 %collective-permute-done.3 = f32[4,136,128]{2,1,0:T(8,128)S(1)} collective-permute-done((f32[4,136,128]{2,1,0:T(8,128)S(1)}, f32[4,136,128]{2,1,0:T(8,128)S(1)}, u32[]{:S(2)}, u32[]{:S(2)}) %collective-permute-start.3) | collective-permute-done | bytes 278560 | tf_op jit(solution)/shard_map/ppermute | solution.py:23
  55.4 0.1 exponential_reduce_fusion.1
  55.5 0.1 multiply_add_fusion
  55.8 1.3 collective-permute-start.4
  57.1 0.6 fusion.1
  57.7 8.0 %collective-permute-done.4 = f32[4,136,128]{2,1,0:T(8,128)S(1)} collective-permute-done((f32[4,136,128]{2,1,0:T(8,128)S(1)}, f32[4,136,128]{2,1,0:T(8,128)S(1)}, u32[]{:S(2)}, u32[]{:S(2)}) %collective-permute-start.4) | collective-permute-done | bytes 278560 | tf_op jit(solution)/shard_map/ppermute | solution.py:23
  65.7 0.8 multiply_reduce_fusion
  66.5 11.5 %collective-permute-start.10 = (f32[256]{0:T(256)S(1)}, f32[256]{0:T(256)S(1)}, u32[]{:S(2)}, u32[]{:S(2)}) collective-permute-start(f32[256]{0:T(256)S(1)} %get-tuple-element.51), channel_id=1, source_target_pairs={{0,6},{1,7},{2,8},{3,9},{4,10},{5,11},{6,12},{7,13},{8,14},{9,15},... | collective-permute-start | bytes 3080 | tf_op jit(solution)/shard_map/ppermute | solution.py:81
  78.0 12.0 %collective-permute-start.11 = (f32[256]{0:T(256)S(1)}, f32[256]{0:T(256)S(1)}, u32[]{:S(2)}, u32[]{:S(2)}) collective-permute-start(f32[256]{0:T(256)S(1)} %get-tuple-element.51), channel_id=1, source_target_pairs={{0,7},{1,8},{2,9},{3,10},{4,11},{5,12},{6,13},{7,14},{8,15},{9,0},... | collective-permute-start | bytes 3080 | tf_op jit(solution)/shard_map/ppermute | solution.py:81
  90.1 2.5 %collective-permute-start.12 = (f32[256]{0:T(256)S(1)}, f32[256]{0:T(256)S(1)}, u32[]{:S(2)}, u32[]{:S(2)}) collective-permute-start(f32[256]{0:T(256)S(1)} %get-tuple-element.51), channel_id=1, source_target_pairs={{0,8},{1,9},{2,10},{3,11},{4,12},{5,13},{6,14},{7,15},{8,0},{9,1},... | collective-permute-start | bytes 3080 | tf_op jit(solution)/shard_map/ppermute | solution.py:81
  92.6 11.6 %collective-permute-start.13 = (f32[256]{0:T(256)S(1)}, f32[256]{0:T(256)S(1)}, u32[]{:S(2)}, u32[]{:S(2)}) collective-permute-start(f32[256]{0:T(256)S(1)} %get-tuple-element.51), channel_id=1, source_target_pairs={{0,9},{1,10},{2,11},{3,12},{4,13},{5,14},{6,15},{7,0},{8,1},{9,2},... | collective-permute-start | bytes 3080 | tf_op jit(solution)/shard_map/ppermute | solution.py:81
  104.3 4.2 %collective-permute-start.14 = (f32[256]{0:T(256)S(1)}, f32[256]{0:T(256)S(1)}, u32[]{:S(2)}, u32[]{:S(2)}) collective-permute-start(f32[256]{0:T(256)S(1)} %get-tuple-element.51), channel_id=1, source_target_pairs={{0,10},{1,11},{2,12},{3,13},{4,14},{5,15},{6,0},{7,1},{8,2},{9,3},... | collective-permute-start | bytes 3080 | tf_op jit(solution)/shard_map/ppermute | solution.py:81
  108.5 3.6 %collective-permute-start.15 = (f32[256]{0:T(256)S(1)}, f32[256]{0:T(256)S(1)}, u32[]{:S(2)}, u32[]{:S(2)}) collective-permute-start(f32[256]{0:T(256)S(1)} %get-tuple-element.51), channel_id=1, source_target_pairs={{0,11},{1,12},{2,13},{3,14},{4,15},{5,0},{6,1},{7,2},{8,3},{9,4},{... | collective-permute-start | bytes 3080 | tf_op jit(solution)/shard_map/ppermute | solution.py:81
  112.1 8.4 %collective-permute-start.16 = (f32[256]{0:T(256)S(1)}, f32[256]{0:T(256)S(1)}, u32[]{:S(2)}, u32[]{:S(2)}) collective-permute-start(f32[256]{0:T(256)S(1)} %get-tuple-element.51), channel_id=1, source_target_pairs={{0,12},{1,13},{2,14},{3,15},{4,0},{5,1},{6,2},{7,3},{8,4},{9,5},{1... | collective-permute-start | bytes 3080 | tf_op jit(solution)/shard_map/ppermute | solution.py:81
  120.5 5.3 %collective-permute-start.17 = (f32[256]{0:T(256)S(1)}, f32[256]{0:T(256)S(1)}, u32[]{:S(2)}, u32[]{:S(2)}) collective-permute-start(f32[256]{0:T(256)S(1)} %get-tuple-element.51), channel_id=1, source_target_pairs={{0,13},{1,14},{2,15},{3,0},{4,1},{5,2},{6,3},{7,4},{8,5},{9,6},{10... | collective-permute-start | bytes 3080 | tf_op jit(solution)/shard_map/ppermute | solution.py:81
  125.9 3.3 %collective-permute-start.18 = (f32[256]{0:T(256)S(1)}, f32[256]{0:T(256)S(1)}, u32[]{:S(2)}, u32[]{:S(2)}) collective-permute-start(f32[256]{0:T(256)S(1)} %get-tuple-element.51), channel_id=1, source_target_pairs={{0,14},{1,15},{2,0},{3,1},{4,2},{5,3},{6,4},{7,5},{8,6},{9,7},{10,... | collective-permute-start | bytes 3080 | tf_op jit(solution)/shard_map/ppermute | solution.py:81
  129.2 2.2 %collective-permute-start.19 = (f32[256]{0:T(256)S(1)}, f32[256]{0:T(256)S(1)}, u32[]{:S(2)}, u32[]{:S(2)}) collective-permute-start(f32[256]{0:T(256)S(1)} %get-tuple-element.51), channel_id=1, source_target_pairs={{0,15},{1,0},{2,1},{3,2},{4,3},{5,4},{6,5},{7,6},{8,7},{9,8},{10,9... | collective-permute-start | bytes 3080 | tf_op jit(solution)/shard_map/ppermute | solution.py:81
  131.4 3.6 %collective-permute-start.5 = (f32[256]{0:T(256)S(1)}, f32[256]{0:T(256)S(1)}, u32[]{:S(2)}, u32[]{:S(2)}) collective-permute-start(f32[256]{0:T(256)S(1)} %get-tuple-element.51), channel_id=1, source_target_pairs={{0,1},{1,2},{2,3},{3,4},{4,5},{5,6},{6,7},{7,8},{8,9},{9,10},{10,1... | collective-permute-start | bytes 3080 | tf_op jit(solution)/shard_map/ppermute | solution.py:81
  135.1 3.4 %collective-permute-start.6 = (f32[256]{0:T(256)S(1)}, f32[256]{0:T(256)S(1)}, u32[]{:S(2)}, u32[]{:S(2)}) collective-permute-start(f32[256]{0:T(256)S(1)} %get-tuple-element.51), channel_id=1, source_target_pairs={{0,2},{1,3},{2,4},{3,5},{4,6},{5,7},{6,8},{7,9},{8,10},{9,11},{10,... | collective-permute-start | bytes 3080 | tf_op jit(solution)/shard_map/ppermute | solution.py:81
  138.5 3.5 %collective-permute-start.7 = (f32[256]{0:T(256)S(1)}, f32[256]{0:T(256)S(1)}, u32[]{:S(2)}, u32[]{:S(2)}) collective-permute-start(f32[256]{0:T(256)S(1)} %get-tuple-element.51), channel_id=1, source_target_pairs={{0,3},{1,4},{2,5},{3,6},{4,7},{5,8},{6,9},{7,10},{8,11},{9,12},{10... | collective-permute-start | bytes 3080 | tf_op jit(solution)/shard_map/ppermute | solution.py:81
  142.1 1.9 %collective-permute-start.8 = (f32[256]{0:T(256)S(1)}, f32[256]{0:T(256)S(1)}, u32[]{:S(2)}, u32[]{:S(2)}) collective-permute-start(f32[256]{0:T(256)S(1)} %get-tuple-element.51), channel_id=1, source_target_pairs={{0,4},{1,5},{2,6},{3,7},{4,8},{5,9},{6,10},{7,11},{8,12},{9,13},{1... | collective-permute-start | bytes 3080 | tf_op jit(solution)/shard_map/ppermute | solution.py:81
  144.0 7.1 %collective-permute-start.9 = (f32[256]{0:T(256)S(1)}, f32[256]{0:T(256)S(1)}, u32[]{:S(2)}, u32[]{:S(2)}) collective-permute-start(f32[256]{0:T(256)S(1)} %get-tuple-element.51), channel_id=1, source_target_pairs={{0,5},{1,6},{2,7},{3,8},{4,9},{5,10},{6,11},{7,12},{8,13},{9,14},{... | collective-permute-start | bytes 3080 | tf_op jit(solution)/shard_map/ppermute | solution.py:81
  151.1 0.7 copy_bitcast_fusion
  151.8 0.2 copy.76
  152.1 3.4 %collective-permute-done.9 = f32[256]{0:T(256)S(1)} collective-permute-done((f32[256]{0:T(256)S(1)}, f32[256]{0:T(256)S(1)}, u32[]{:S(2)}, u32[]{:S(2)}) %collective-permute-start.9) | collective-permute-done | bytes 1056 | tf_op jit(solution)/shard_map/ppermute | solution.py:81
  155.5 0.8 multiply_convert_fusion
  156.3 23.1 %shard_map.95 = bf16[256,512]{1,0:T(8,128)(2,1)} custom-call(s32[1]{0:T(128)} %bitcast.11.index_ref, bf16[1024,128]{1,0:T(8,128)(2,1)} %bitcast.84, bf16[256,8192]{1,0:T(8,128)(2,1)} %bitcast.82), custom_call_target="tpu_custom_call" | custom-call | tf_op jit(solution)/shard_map/pallas_call | solution.py:147
  (48 shorter events, 1.3 us)
Async XLA Ops:
  7.2 41.1 %copy-start = (bf16[256,512]{1,0:T(8,128)(2,1)S(1)}, bf16[256,512]{1,0:T(8,128)(2,1)}, u32[]{:S(2)}) copy-start(bf16[256,512]{1,0:T(8,128)(2,1)} %param.8) | copy-start | bytes 786436
  7.2 149.2 %all-gather.2.cloned.1.call-start = ((), (), s32[]{:S(2)}) async-start(), calls=%async_computation | async-start | bytes 4325376 | tf_op jit(solution)/shard_map/all_gather | solution.py:173
  14.0 43.1 %copy-start.2 = (bf16[256,512]{1,0:T(8,128)(2,1)S(1)}, bf16[256,512]{1,0:T(8,128)(2,1)}, u32[]{:S(2)}) copy-start(bf16[256,512]{1,0:T(8,128)(2,1)} %param.10) | copy-start | bytes 786436
  14.0 10.1 %collective-permute-start = (f32[4,136,128]{2,1,0:T(8,128)S(1)}, f32[4,136,128]{2,1,0:T(8,128)S(1)}, u32[]{:S(2)}, u32[]{:S(2)}) collective-permute-start(f32[4,136,128]{2,1,0:T(8,128)S(1)} %pad_maximum_fusion), channel_id=1, source_target_pairs={{0,16},{16,32},{32,48},{48,64},{64,80},{80,96},{96,112},{112,128},... | collective-permute-start | bytes 835592 | tf_op jit(solution)/shard_map/ppermute | solution.py:23
  24.4 10.6 %collective-permute-start.1 = (f32[4,136,128]{2,1,0:T(8,128)S(1)}, f32[4,136,128]{2,1,0:T(8,128)S(1)}, u32[]{:S(2)}, u32[]{:S(2)}) collective-permute-start(f32[4,136,128]{2,1,0:T(8,128)S(1)} %pad_maximum_fusion.1), channel_id=1, source_target_pairs={{0,32},{16,48},{32,64},{48,80},{64,96},{80,112},{96,128},{112,144}... | collective-permute-start | bytes 835592 | tf_op jit(solution)/shard_map/ppermute | solution.py:23
  35.3 11.3 %collective-permute-start.2 = (f32[4,136,128]{2,1,0:T(8,128)S(1)}, f32[4,136,128]{2,1,0:T(8,128)S(1)}, u32[]{:S(2)}, u32[]{:S(2)}) collective-permute-start(f32[4,136,128]{2,1,0:T(8,128)S(1)} %pad_maximum_fusion.2), channel_id=1, source_target_pairs={{0,64},{16,80},{32,96},{48,112},{64,128},{80,144},{96,160},{112,17... | collective-permute-start | bytes 835592 | tf_op jit(solution)/shard_map/ppermute | solution.py:23
  46.9 104.2 %copy-start.1 = (bf16[256,512]{1,0:T(8,128)(2,1)S(1)}, bf16[256,512]{1,0:T(8,128)(2,1)}, u32[]{:S(2)}) copy-start(bf16[256,512]{1,0:T(8,128)(2,1)} %param.13) | copy-start | bytes 786436
  47.0 8.4 %collective-permute-start.3 = (f32[4,136,128]{2,1,0:T(8,128)S(1)}, f32[4,136,128]{2,1,0:T(8,128)S(1)}, u32[]{:S(2)}, u32[]{:S(2)}) collective-permute-start(f32[4,136,128]{2,1,0:T(8,128)S(1)} %pad_maximum_fusion.3), channel_id=1, source_target_pairs={{0,128},{16,144},{32,160},{48,176},{64,192},{80,208},{96,224},{112... | collective-permute-start | bytes 835592 | tf_op jit(solution)/shard_map/ppermute | solution.py:23
  49.0 106.5 %copy-start.3 = (f32[512]{0:T(512)S(1)}, f32[512]{0:T(512)}, u32[]{:S(2)}) copy-start(f32[512]{0:T(512)} %param.12) | copy-start | bytes 6148
  55.8 9.9 %collective-permute-start.4 = (f32[4,136,128]{2,1,0:T(8,128)S(1)}, f32[4,136,128]{2,1,0:T(8,128)S(1)}, u32[]{:S(2)}, u32[]{:S(2)}) collective-permute-start(f32[4,136,128]{2,1,0:T(8,128)S(1)} %pad_maximum_fusion.4), channel_id=1, source_target_pairs={{0,256},{16,272},{32,288},{48,304},{64,320},{80,336},{96,352},{112... | collective-permute-start | bytes 835592 | tf_op jit(solution)/shard_map/ppermute | solution.py:23
  66.5 41.9 %collective-permute-start.10 = (f32[256]{0:T(256)S(1)}, f32[256]{0:T(256)S(1)}, u32[]{:S(2)}, u32[]{:S(2)}) collective-permute-start(f32[256]{0:T(256)S(1)} %get-tuple-element.51), channel_id=1, source_target_pairs={{0,6},{1,7},{2,8},{3,9},{4,10},{5,11},{6,12},{7,13},{8,14},{9,15},... | collective-permute-start | bytes 3080 | tf_op jit(solution)/shard_map/ppermute | solution.py:81
  78.0 34.1 %collective-permute-start.11 = (f32[256]{0:T(256)S(1)}, f32[256]{0:T(256)S(1)}, u32[]{:S(2)}, u32[]{:S(2)}) collective-permute-start(f32[256]{0:T(256)S(1)} %get-tuple-element.51), channel_id=1, source_target_pairs={{0,7},{1,8},{2,9},{3,10},{4,11},{5,12},{6,13},{7,14},{8,15},{9,0},... | collective-permute-start | bytes 3080 | tf_op jit(solution)/shard_map/ppermute | solution.py:81
  90.1 30.4 %collective-permute-start.12 = (f32[256]{0:T(256)S(1)}, f32[256]{0:T(256)S(1)}, u32[]{:S(2)}, u32[]{:S(2)}) collective-permute-start(f32[256]{0:T(256)S(1)} %get-tuple-element.51), channel_id=1, source_target_pairs={{0,8},{1,9},{2,10},{3,11},{4,12},{5,13},{6,14},{7,15},{8,0},{9,1},... | collective-permute-start | bytes 3080 | tf_op jit(solution)/shard_map/ppermute | solution.py:81
  92.6 33.3 %collective-permute-start.13 = (f32[256]{0:T(256)S(1)}, f32[256]{0:T(256)S(1)}, u32[]{:S(2)}, u32[]{:S(2)}) collective-permute-start(f32[256]{0:T(256)S(1)} %get-tuple-element.51), channel_id=1, source_target_pairs={{0,9},{1,10},{2,11},{3,12},{4,13},{5,14},{6,15},{7,0},{8,1},{9,2},... | collective-permute-start | bytes 3080 | tf_op jit(solution)/shard_map/ppermute | solution.py:81
  104.3 24.9 %collective-permute-start.14 = (f32[256]{0:T(256)S(1)}, f32[256]{0:T(256)S(1)}, u32[]{:S(2)}, u32[]{:S(2)}) collective-permute-start(f32[256]{0:T(256)S(1)} %get-tuple-element.51), channel_id=1, source_target_pairs={{0,10},{1,11},{2,12},{3,13},{4,14},{5,15},{6,0},{7,1},{8,2},{9,3},... | collective-permute-start | bytes 3080 | tf_op jit(solution)/shard_map/ppermute | solution.py:81
  108.5 23.0 %collective-permute-start.15 = (f32[256]{0:T(256)S(1)}, f32[256]{0:T(256)S(1)}, u32[]{:S(2)}, u32[]{:S(2)}) collective-permute-start(f32[256]{0:T(256)S(1)} %get-tuple-element.51), channel_id=1, source_target_pairs={{0,11},{1,12},{2,13},{3,14},{4,15},{5,0},{6,1},{7,2},{8,3},{9,4},{... | collective-permute-start | bytes 3080 | tf_op jit(solution)/shard_map/ppermute | solution.py:81
  112.1 23.0 %collective-permute-start.16 = (f32[256]{0:T(256)S(1)}, f32[256]{0:T(256)S(1)}, u32[]{:S(2)}, u32[]{:S(2)}) collective-permute-start(f32[256]{0:T(256)S(1)} %get-tuple-element.51), channel_id=1, source_target_pairs={{0,12},{1,13},{2,14},{3,15},{4,0},{5,1},{6,2},{7,3},{8,4},{9,5},{1... | collective-permute-start | bytes 3080 | tf_op jit(solution)/shard_map/ppermute | solution.py:81
  120.5 18.0 %collective-permute-start.17 = (f32[256]{0:T(256)S(1)}, f32[256]{0:T(256)S(1)}, u32[]{:S(2)}, u32[]{:S(2)}) collective-permute-start(f32[256]{0:T(256)S(1)} %get-tuple-element.51), channel_id=1, source_target_pairs={{0,13},{1,14},{2,15},{3,0},{4,1},{5,2},{6,3},{7,4},{8,5},{9,6},{10... | collective-permute-start | bytes 3080 | tf_op jit(solution)/shard_map/ppermute | solution.py:81
  125.9 16.2 %collective-permute-start.18 = (f32[256]{0:T(256)S(1)}, f32[256]{0:T(256)S(1)}, u32[]{:S(2)}, u32[]{:S(2)}) collective-permute-start(f32[256]{0:T(256)S(1)} %get-tuple-element.51), channel_id=1, source_target_pairs={{0,14},{1,15},{2,0},{3,1},{4,2},{5,3},{6,4},{7,5},{8,6},{9,7},{10,... | collective-permute-start | bytes 3080 | tf_op jit(solution)/shard_map/ppermute | solution.py:81
  129.2 14.8 %collective-permute-start.19 = (f32[256]{0:T(256)S(1)}, f32[256]{0:T(256)S(1)}, u32[]{:S(2)}, u32[]{:S(2)}) collective-permute-start(f32[256]{0:T(256)S(1)} %get-tuple-element.51), channel_id=1, source_target_pairs={{0,15},{1,0},{2,1},{3,2},{4,3},{5,4},{6,5},{7,6},{8,7},{9,8},{10,9... | collective-permute-start | bytes 3080 | tf_op jit(solution)/shard_map/ppermute | solution.py:81
  131.4 20.6 %collective-permute-start.5 = (f32[256]{0:T(256)S(1)}, f32[256]{0:T(256)S(1)}, u32[]{:S(2)}, u32[]{:S(2)}) collective-permute-start(f32[256]{0:T(256)S(1)} %get-tuple-element.51), channel_id=1, source_target_pairs={{0,1},{1,2},{2,3},{3,4},{4,5},{5,6},{6,7},{7,8},{8,9},{9,10},{10,1... | collective-permute-start | bytes 3080 | tf_op jit(solution)/shard_map/ppermute | solution.py:81
  135.1 17.0 %collective-permute-start.6 = (f32[256]{0:T(256)S(1)}, f32[256]{0:T(256)S(1)}, u32[]{:S(2)}, u32[]{:S(2)}) collective-permute-start(f32[256]{0:T(256)S(1)} %get-tuple-element.51), channel_id=1, source_target_pairs={{0,2},{1,3},{2,4},{3,5},{4,6},{5,7},{6,8},{7,9},{8,10},{9,11},{10,... | collective-permute-start | bytes 3080 | tf_op jit(solution)/shard_map/ppermute | solution.py:81
  138.5 13.5 %collective-permute-start.7 = (f32[256]{0:T(256)S(1)}, f32[256]{0:T(256)S(1)}, u32[]{:S(2)}, u32[]{:S(2)}) collective-permute-start(f32[256]{0:T(256)S(1)} %get-tuple-element.51), channel_id=1, source_target_pairs={{0,3},{1,4},{2,5},{3,6},{4,7},{5,8},{6,9},{7,10},{8,11},{9,12},{10... | collective-permute-start | bytes 3080 | tf_op jit(solution)/shard_map/ppermute | solution.py:81
  142.1 10.0 %collective-permute-start.8 = (f32[256]{0:T(256)S(1)}, f32[256]{0:T(256)S(1)}, u32[]{:S(2)}, u32[]{:S(2)}) collective-permute-start(f32[256]{0:T(256)S(1)} %get-tuple-element.51), channel_id=1, source_target_pairs={{0,4},{1,5},{2,6},{3,7},{4,8},{5,9},{6,10},{7,11},{8,12},{9,13},{1... | collective-permute-start | bytes 3080 | tf_op jit(solution)/shard_map/ppermute | solution.py:81
  144.0 11.5 %collective-permute-start.9 = (f32[256]{0:T(256)S(1)}, f32[256]{0:T(256)S(1)}, u32[]{:S(2)}, u32[]{:S(2)}) collective-permute-start(f32[256]{0:T(256)S(1)} %get-tuple-element.51), channel_id=1, source_target_pairs={{0,5},{1,6},{2,7},{3,8},{4,9},{5,10},{6,11},{7,12},{8,13},{9,14},{... | collective-permute-start | bytes 3080 | tf_op jit(solution)/shard_map/ppermute | solution.py:81
Sparse Core Ops, SparseCore 0:
  11.6 72.4 all-gather.1
